TPU v7x, 128 devices: a whole 4x4x4 slice. The times are simulated.
128 devices in a mesh: pool: 4 (over x_hi, core), grp: 4 (over y), tp: 8 (over z, x_lo).
Axes of the slice: x: 4 (x_hi: 2, x_lo: 2; x = x_hi * 2 + x_lo), y: 4, z: 4, core: 2. Of those that a mesh axis runs over, the one named last changes fastest.
Arguments:
- hidden: bfloat16 [1024, 8192], P('pool', 'grp'), may hold values from -6 to 6
- attn_gain: float32 [8192], P('grp'), may hold values from 0.25 to 1.75
- w_query: bfloat16 [8192, 8192], P('grp', 'tp'), may hold values from -0.0625 to 0.0625
- w_key: bfloat16 [8192, 1024], P('grp', 'tp'), may hold values from -1 to 1
- w_value: bfloat16 [8192, 1024], P('grp', 'tp'), may hold values from -0.0625 to 0.0625
- w_out: bfloat16 [8192, 8192], P('tp', 'grp'), may hold values from -0.0625 to 0.0625
- prefix_keys: bfloat16 [8, 16384, 1024], P('pool', 'grp', 'tp'), may hold values from -300 to 300
- prefix_values: bfloat16 [8, 16384, 1024], P('pool', 'grp', 'tp'), may hold values from -6 to 6
- suffix_keys: bfloat16 [1024, 256, 1024], P('pool', 'grp', 'tp'), may hold values from -300 to 300
- suffix_values: bfloat16 [1024, 256, 1024], P('pool', 'grp', 'tp'), may hold values from -6 to 6
- prefix_ids: int32 [1024], P('pool'), may hold values from 0 to 7, as said below
- suffix_lens: int32 [1024], P('pool'), may hold values from 1 to 256, as said below
- ffn_gain: float32 [8192], P('grp'), may hold values from 0.25 to 1.75
- w_gate: bfloat16 [8192, 14336], P('grp', ('pool', 'tp')), may hold values from -0.0625 to 0.0625
- w_up: bfloat16 [8192, 14336], P('grp', ('pool', 'tp')), may hold values from -0.0625 to 0.0625
- w_down: bfloat16 [14336, 8192], P(('pool', 'tp'), 'grp'), may hold values from -0.046875 to 0.046875
Outputs:
- result: bfloat16 [1024, 8192], P(('pool', 'tp'), 'grp')
Inputs may be any that keep to these rules, and one draw needn't show every extreme that they name: `prefix_ids`: within rows p * 256 to (p + 1) * 256 - 1, each of the prefixes p * 2 to (p + 1) * 2 - 1 is named by exactly 128 streams, and no other prefix is named. `suffix_lens`: each block of 256 streams holds a stream of length 256 and one of length 1.
All inputs are finite; a program needn't handle non-finite values.
Results may differ from a plain program's by a relative error of at most 0.015.
Values may be sent and summed in bfloat16 or wider, within the bound.
No kernel may reach another device: no remote copies, remote signals or barrier semaphores. Data moves between devices by JAX's collectives and lax.ppermute only.
A program may use at most 192 MiB of HBM per device.

v0:
```python
import math

import jax
import jax.numpy as jnp
from jax import lax
from jax.sharding import PartitionSpec as P

D = 8192
HD = 128


epsilon = 1e-05


def joined(array, axis, combine):
    everything = jax.tree.map(lambda part: lax.all_gather(part, axis), array)
    first = jax.tree.map(lambda part: part[0], everything)

    def lap(k, so_far):
        return combine(so_far, jax.tree.map(lambda part: part[k], everything))

    return lax.fori_loop(1, lax.axis_size(axis), lap, first)


def combine_parts(earlier, later):
    peak_one, total_one, numer_one = earlier
    peak_two, total_two, numer_two = later
    peak = jnp.maximum(peak_one, peak_two)
    scale_one = jnp.exp(peak_one - peak)
    scale_two = jnp.exp(peak_two - peak)
    total = total_one * scale_one + total_two * scale_two
    numer = numer_one * scale_one[..., None] + numer_two * scale_two[..., None]
    return (peak, total, numer)


def body(
    hidden,
    attn_gain,
    w_query,
    w_key,
    w_value,
    w_out,
    prefix_keys,
    prefix_values,
    suffix_keys,
    suffix_values,
    prefix_ids,
    suffix_lens,
    ffn_gain,
    w_gate,
    w_up,
    w_down,
):
    stream_count = hidden.shape[0]
    hidden_float = hidden.astype(jnp.float32)
    squares = lax.psum(jnp.sum(hidden_float * hidden_float, axis=1), "grp")
    inverse = lax.rsqrt(squares / D + epsilon)
    normed = (hidden_float * inverse[:, None] * attn_gain).astype(jnp.bfloat16)
    part_query = jnp.dot(normed, w_query, preferred_element_type=jnp.float32)
    part_key = jnp.dot(normed, w_key, preferred_element_type=jnp.float32)
    part_value = jnp.dot(normed, w_value, preferred_element_type=jnp.float32)
    query, key_new, value_new = lax.psum((part_query, part_key, part_value), "grp")
    query = query.astype(jnp.bfloat16)
    key_new = key_new.astype(jnp.bfloat16)
    value_new = value_new.astype(jnp.bfloat16)
    kv_local = w_key.shape[1] // HD
    q_local = w_query.shape[1] // HD
    groups = q_local // kv_local
    prefix_local = prefix_keys.shape[0]
    pre_length = prefix_keys.shape[1]
    suf_length = suffix_keys.shape[1]
    factor = 1.0 / math.sqrt(HD)
    heads = query.reshape(stream_count, kv_local, groups, HD)
    pre_key = prefix_keys.reshape(prefix_local, pre_length, kv_local, HD)
    pre_value = prefix_values.reshape(prefix_local, pre_length, kv_local, HD)
    suf_key = suffix_keys.reshape(stream_count, suf_length, kv_local, HD)
    suf_value = suffix_values.reshape(stream_count, suf_length, kv_local, HD)
    local_prefix = prefix_ids - lax.axis_index("pool") * prefix_local
    per_group = stream_count // prefix_local
    one_hot = (local_prefix[:, None] == jnp.arange(prefix_local, dtype=jnp.int32)[None, :]).astype(
        jnp.int32
    )
    rank_within = jnp.sum(jnp.cumsum(one_hot, axis=0) * one_hot, axis=1) - 1
    target = local_prefix * per_group + rank_within
    group_order = (
        jnp.zeros((stream_count,), jnp.int32)
        .at[target]
        .set(jnp.arange(stream_count, dtype=jnp.int32))
    )
    grouped = heads[group_order].reshape(prefix_local, per_group, kv_local, groups, HD)
    pre_scores = (
        jnp.einsum("pskgd,pjkd->pskgj", grouped, pre_key, preferred_element_type=jnp.float32)
        * factor
    )
    pre_peak = pre_scores.max(axis=4).reshape(stream_count, kv_local, groups)[target]
    positions = lax.axis_index("grp") * suf_length + jnp.arange(suf_length, dtype=jnp.int32)
    valid = (positions[None, :] < suffix_lens[:, None])[:, None, None, :]
    suf_scores = (
        jnp.einsum("skgd,sjkd->skgj", heads, suf_key, preferred_element_type=jnp.float32) * factor
    )
    suf_scores = jnp.where(valid, suf_scores, -1e30)
    peak = jnp.maximum(pre_peak, suf_scores.max(axis=3))
    peak_grouped = peak[group_order].reshape(prefix_local, per_group, kv_local, groups)
    pre_weights = jnp.exp(pre_scores - peak_grouped[..., None]).astype(jnp.bfloat16)
    pre_total = (
        pre_weights.astype(jnp.float32).sum(axis=4).reshape(stream_count, kv_local, groups)[target]
    )
    pre_numer = jnp.einsum(
        "pskgj,pjkd->pskgd", pre_weights, pre_value, preferred_element_type=jnp.float32
    )
    pre_numer = pre_numer.reshape(stream_count, kv_local, groups, HD)[target]
    suf_weights = jnp.where(valid, jnp.exp(suf_scores - peak[:, :, :, None]), 0.0).astype(
        jnp.bfloat16
    )
    total = pre_total + suf_weights.astype(jnp.float32).sum(axis=3)
    numer = pre_numer + jnp.einsum(
        "skgj,sjkd->skgd", suf_weights, suf_value, preferred_element_type=jnp.float32
    )
    peak, total, numer = joined((peak, total, numer), "grp", combine_parts)
    own_score = (
        jnp.einsum(
            "skgd,skd->skg",
            heads,
            key_new.reshape(stream_count, kv_local, HD),
            preferred_element_type=jnp.float32,
        )
        * factor
    )
    new_peak = jnp.maximum(peak, own_score)
    rescale = jnp.exp(peak - new_peak)
    own_weight = jnp.exp(own_score - new_peak).astype(jnp.bfloat16).astype(jnp.float32)
    total = total * rescale + own_weight
    own_value = value_new.reshape(stream_count, kv_local, 1, HD).astype(jnp.float32)
    numer = numer * rescale[..., None] + own_weight[..., None] * own_value
    attended = (numer / total[..., None]).reshape(stream_count, q_local * HD).astype(jnp.bfloat16)
    partial_out = jnp.dot(attended, w_out, preferred_element_type=jnp.float32)
    share = stream_count // lax.axis_size("tp")
    tp_start = lax.axis_index("tp") * share
    summed = lax.psum(partial_out, "tp")
    summed = lax.dynamic_slice_in_dim(summed, tp_start, share, 0)
    own_hidden = lax.dynamic_slice_in_dim(hidden_float, tp_start, share, 0)
    middle = (own_hidden + summed).astype(jnp.bfloat16)
    gathered = lax.all_gather(middle, ("pool", "tp"), axis=0, tiled=True)
    gathered_float = gathered.astype(jnp.float32)
    ffn_squares = lax.psum(jnp.sum(gathered_float * gathered_float, axis=1), "grp")
    ffn_inverse = lax.rsqrt(ffn_squares / D + epsilon)
    normed_ffn = (gathered_float * ffn_inverse[:, None] * ffn_gain).astype(jnp.bfloat16)
    part_gate = jnp.dot(normed_ffn, w_gate, preferred_element_type=jnp.float32)
    part_upward = jnp.dot(normed_ffn, w_up, preferred_element_type=jnp.float32)
    gate, upward = lax.psum((part_gate, part_upward), "grp")
    act = (jax.nn.silu(gate) * upward).astype(jnp.bfloat16)
    returned = lax.psum_scatter(
        jnp.dot(act, w_down, preferred_element_type=jnp.float32),
        ("pool", "tp"),
        scatter_dimension=0,
        tiled=True,
    )
    return (middle.astype(jnp.float32) + returned).astype(jnp.bfloat16)


def solution(mesh):
    return jax.shard_map(
        body,
        mesh=mesh,
        in_specs=(
            P("pool", "grp"),
            P("grp"),
            P("grp", "tp"),
            P("grp", "tp"),
            P("grp", "tp"),
            P("tp", "grp"),
            P("pool", "grp", "tp"),
            P("pool", "grp", "tp"),
            P("pool", "grp", "tp"),
            P("pool", "grp", "tp"),
            P("pool"),
            P("pool"),
            P("grp"),
            P("grp", ("pool", "tp")),
            P("grp", ("pool", "tp")),
            P(("pool", "tp"), "grp"),
        ),
        out_specs=P(("pool", "tp"), "grp"),
        check_vma=False,
    )
```

profile of v0, /device:TPU:0, one launch (start us, length us, event | category | flops | bytes accessed | tf_op | source)
XLA Modules:
  0.0 672.1 jit_solution(15598244335575411505)
XLA Ops:
  9.7 10.9 %psum.56 = f32[256]{0:T(256)S(1)} all-reduce(f32[256]{0:T(256)S(1)} %multiply_reduce_fusion), channel_id=1, replica_groups=mesh['pool'=4,'grp'=4,'tp'=8] {'grp'}, use_global_device_ids=true, to_apply=%region_1.0 | all-reduce | flops 256 | bytes 2048 | tf_op jit(solution)/shard_map/psum | solution.py:56
  20.5 4.9 fusion.46
  26.5 30.8 %all-reduce.9 = (bf16[256,1024]{1,0:T(8,128)(2,1)S(1)}, bf16[256,128]{1,0:T(8,128)(2,1)S(1)}, bf16[256,128]{1,0:T(8,128)(2,1)S(1)}) all-reduce(f32[256,1024]{1,0:T(8,128)} %fusion.46, f32[256,128]{1,0:T(8,128)S(1)} %fusion.45, f32[256,128]{1,0:T(8,128)S(1)} %fusion.44), channel_id=1, replica_groups=mesh['pool'=4,'grp'=4,'tp'=8] {'grp'}, use_global_device_ids=true, to_apply=%region_2.0 | all-reduce | flops 327680 | bytes 1966080 | tf_op jit(solution)/shard_map/psum | solution.py:62
  61.0 13.1 %bitcast_reduce_fusion = (f32[2,128,8]{1,2,0:T(8,128)S(1)}, f32[2,128,8,4096]{3,1,2,0:T(8,128)}) fusion(bf16[2,4096,128]{2,1,0:T(8,128)(2,1)S(1)} %copy-done, bf16[2,128,8,128]{3,2,1,0:T(8,128)(2,1)S(1)} %bitcast.165), kind=kOutput, calls=%fused_computation.17 | convolution fusion | flops 2164258816 | bytes 36184064 | tf_op jit(solution)/shard_map/pskgd,pjkd->pskgj/dot_general | solution.py:92
  75.1 4.5 fusion.47
  80.4 13.8 %fusion.17 = f32[2,128,1,8,128]{4,1,3,0,2:T(8,128)S(1)} fusion(bf16[2,4096,128]{2,1,0:T(8,128)(2,1)} %param.25, f32[2,128,8]{1,2,0:T(8,128)S(1)} %copy.48, f32[2,128,8,4096]{3,1,2,0:T(8,128)} %get-tuple-element.234), kind=kOutput, calls=%fused_computation.37 | convolution fusion | flops 2172649472 | bytes 36708352 | tf_op jit(solution)/shard_map/pskgj,pjkd->pskgd/dot_general | solution.py:108
  95.9 2.9 gather_fusion.4
  98.8 4.7 convolution_add_fusion
  103.6 12.8 %all-gather.1 = f32[1024,8]{1,0:T(8,128)S(1)} all-gather(f32[256,8]{1,0:T(8,128)S(1)} %max.43), channel_id=3, replica_groups=mesh['pool'=4,'grp'=4,'tp'=8] {'grp'}, dimensions={0}, use_global_device_ids=true | all-gather | bytes 40960 | tf_op jit(solution)/shard_map/all_gather | solution.py:16
  116.5 14.2 %convert_reduce_fusion = f32[2,128,8]{1,2,0:T(8,128)S(1)} fusion(f32[2,128,8]{1,2,0:T(8,128)S(1)} %copy.48, f32[2,128,8,4096]{3,1,2,0:T(8,128)} %get-tuple-element.234), kind=kLoop, calls=%fused_computation.20 | loop fusion | flops 41940992 | bytes 33570816 | tf_op jit(solution)/shard_map/reduce_sum | solution.py:106
  132.3 15.5 %all-gather.2 = f32[1024,8]{1,0:T(8,128)S(1)} all-gather(f32[256,8]{1,0:T(8,128)S(1)} %add.162), channel_id=4, replica_groups=mesh['pool'=4,'grp'=4,'tp'=8] {'grp'}, dimensions={0}, use_global_device_ids=true | all-gather | bytes 40960 | tf_op jit(solution)/shard_map/all_gather | solution.py:16
  148.7 8.1 %all-gather.8.cloned.1.call-done = f32[1024,8,128]{2,1,0:T(8,128)} async-done(((f32[256,8,128]{2,1,0:T(8,128)}), f32[1024,8,128]{2,1,0:T(8,128)}) %all-gather.8.cloned.1.call-update) | async-done | bytes 4194320 | tf_op jit(solution)/shard_map/all_gather | solution.py:16
  158.2 6.7 while.19
  158.5 1.9 fusion.65
  166.3 4.8 fusion.28
  172.8 103.7 %all-reduce.6.cloned.1.call-done = f32[256,2048]{1,0:T(8,128)} async-done(((f32[256,2048]{1,0:T(8,128)}), f32[256,2048]{1,0:T(8,128)}) %all-reduce.6.cloned.1.call-update) | async-done | bytes 2097168 | tf_op jit(solution)/shard_map/psum | solution.py:139
  278.3 84.4 %all-gather.6.cloned.1.call-done = bf16[1024,2048]{1,0:T(8,128)(2,1)} async-done(((bf16[32,2048]{1,0:T(8,128)(2,1)}), bf16[1024,2048]{1,0:T(8,128)(2,1)}) %all-gather.6.cloned.1.call-update) | async-done | bytes 4194320 | tf_op jit(solution)/shard_map/all_gather | solution.py:143
  362.8 3.1 fusion.9
  365.8 10.5 %psum.61 = f32[1024]{0:T(1024)S(1)} all-reduce(f32[1024]{0:T(1024)S(1)} %fusion.9), channel_id=1, replica_groups=mesh['pool'=4,'grp'=4,'tp'=8] {'grp'}, use_global_device_ids=true, to_apply=%region_17.18 | all-reduce | flops 1024 | bytes 8192 | tf_op jit(solution)/shard_map/psum | solution.py:145
  376.4 6.4 fusion.22
  382.7 3.5 fusion.24
  386.3 83.8 %all-reduce.8.cloned.1.call-done = (f32[1024,448]{0,1:T(8,128)}, f32[1024,448]{0,1:T(8,128)}) async-done(((f32[1024,448]{0,1:T(8,128)}, f32[1024,448]{0,1:T(8,128)}), (f32[1024,448]{0,1:T(8,128)}, f32[1024,448]{0,1:T(8,128)})) %all-reduce.8.cloned.1.call-update) | async-done | bytes 3670032 | tf_op jit(solution)/shard_map/psum | solution.py:150
  470.1 8.3 %fusion.26 = f32[1024,2048]{1,0:T(8,128)} fusion(bf16[448,2048]{1,0:T(8,128)(2,1)} %param.33, f32[1024,448]{0,1:T(8,128)} %get-tuple-element.224, f32[1024,448]{0,1:T(8,128)} %get-tuple-element.225), kind=kOutput, calls=%fused_computation.44 | convolution fusion | flops 1881800704 | bytes 13893632 | tf_op jit(solution)/shard_map/dot_general | solution.py:153
  478.4 185.6 %reduce-scatter.2.cloned.1.call-done = f32[32,2048]{1,0:T(8,128)} async-done(((f32[1024,2048]{1,0:T(8,128)}), f32[32,2048]{1,0:T(8,128)}) %reduce-scatter.2.cloned.1.call-update) | async-done | bytes 262160 | tf_op jit(solution)/shard_map/reduce_scatter | solution.py:152
  (104 shorter events, 26.2 us)
Async XLA Ops:
  6.5 54.5 %copy-start = (bf16[2,4096,128]{2,1,0:T(8,128)(2,1)S(1)}, bf16[2,4096,128]{2,1,0:T(8,128)(2,1)}, u32[]{:S(2)}) copy-start(bf16[2,4096,128]{2,1,0:T(8,128)(2,1)} %param.24) | copy-start | bytes 6291460
  6.5 150.3 %all-gather.8.cloned.1.call-start = ((), (), s32[]{:S(2)}) async-start(), calls=%async_computation.4 | async-start | bytes 5242880 | tf_op jit(solution)/shard_map/all_gather | solution.py:16
  8.1 17.4 %copy-start.2 = (bf16[256,2048]{1,0:T(8,128)(2,1)S(1)}, bf16[256,2048]{1,0:T(8,128)(2,1)}, u32[]{:S(2)}) copy-start(bf16[256,2048]{1,0:T(8,128)(2,1)} %param.18) | copy-start | bytes 3145732
  8.1 17.4 %copy-start.11 = (f32[2048]{0:T(1024)S(1)}, f32[2048]{0:T(1024)}, u32[]{:S(2)}) copy-start(f32[2048]{0:T(1024)} %param.19) | copy-start | bytes 24580
  20.5 4.9 copy-start.9
  20.5 5.4 copy-start.10
  25.4 33.1 %copy-start.6 = (s32[256]{0:T(256)S(1)}, s32[256]{0:T(256)}, u32[]{:S(2)}) copy-start(s32[256]{0:T(256)} %param.28) | copy-start | bytes 3076
  61.0 14.0 %copy-start.7 = (s32[256]{0:T(256)S(1)}, s32[256]{0:T(256)}, u32[]{:S(2)}) copy-start(s32[256]{0:T(256)} %param.29) | copy-start | bytes 3076
  103.6 173.0 %all-reduce.6.cloned.1.call-start = ((), (), s32[]{:S(2)}) async-start(), calls=%async_computation.1 | async-start | bytes 4194304 | tf_op jit(solution)/shard_map/psum | solution.py:139
  166.3 4.9 copy-start.3
  171.2 205.2 %copy-start.12 = (f32[2048]{0:T(1024)S(1)}, f32[2048]{0:T(1024)}, u32[]{:S(2)}) copy-start(f32[2048]{0:T(1024)} %param.30) | copy-start | bytes 24580
  171.2 191.6 %all-gather.6.cloned.1.call-start = ((), (), s32[]{:S(2)}) async-start(), calls=%async_computation.2 | async-start | bytes 4325376 | tf_op jit(solution)/shard_map/all_gather | solution.py:143
  278.3 191.8 %all-reduce.8.cloned.1.call-start = ((), (), s32[]{:S(2)}) async-start(), calls=%async_computation.5 | async-start | bytes 7340032 | tf_op jit(solution)/shard_map/psum | solution.py:150
  376.3 6.4 copy-start.4
  376.3 6.4 copy-start.8
  386.2 277.7 %reduce-scatter.2.cloned.1.call-start = ((), (), s32[]{:S(2)}) async-start(), calls=%async_computation.3 | async-start | bytes 8650752 | tf_op jit(solution)/shard_map/reduce_scatter | solution.py:152
  478.4 187.2 %copy-start.1 = (bf16[2,4096,128]{2,1,0:T(8,128)(2,1)S(1)}, bf16[2,4096,128]{2,1,0:T(8,128)(2,1)}, u32[]{:S(2)}) copy-start(bf16[2,4096,128]{2,1,0:T(8,128)(2,1)} %param.24) | copy-start | bytes 6291460
  478.4 185.6 %copy-start.5 = (bf16[32,2048]{1,0:T(8,128)(2,1)S(1)}, bf16[32,2048]{1,0:T(8,128)(2,1)}, u32[]{:S(2)}) copy-start(bf16[32,2048]{1,0:T(8,128)(2,1)} %add_convert_fusion.1) | copy-start | bytes 393220
Sparse Core Ops, SparseCore 0:
  103.7 53.1 all-gather.7
  171.3 105.2 all-reduce.5
  278.4 84.3 all-gather.5
  386.3 83.7 all-reduce.7
  478.5 185.3 reduce-scatter.1
where the time goes:
time: 673 us; the launch traced here: 672 us
  waiting for transfers between devices  466 us (69%)
  blocking collectives  80.4 us (12%)
  matrix products  65.4 us (10%)
  other arithmetic  33.9 us (5%)
  between operations  13.5 us (2%)
  local copies, waits for them, and re-layouts  12.8 us (2%)
    reduce_scatter x1, waiting for transfers between devices, body(): lax.psum_scatter(jnp.dot(act, w_down, preferred_element_type=jnp.float32)...  186 us
    psum x1, waiting for transfers between devices, body(): summed = lax.psum(partial_out, 'tp')  104 us
    all_gather x1, waiting for transfers between devices, body(): gathered = lax.all_gather(middle, ('pool', 'tp'), axis=0, tiled=True)  84.4 us
    psum x1, waiting for transfers between devices, body(): gate, upward = lax.psum((part_gate, part_upward), 'grp')  83.8 us
    psum x1, blocking collectives, body(): lax.psum((part_query, part_key, part_value), 'grp')  30.8 us
    all_gather x2, blocking collectives, joined(): everything = jax.tree.map(lambda part: lax.all_gather(part, axis), array)  28.3 us
    reduce_sum x1, other arithmetic, body(): pre_weights.astype(jnp.float32).sum(axis=4)  14.2 us
    dot_general x1, matrix products, body(): jnp.einsum('pskgj,pjkd->pskgd', pre_weights, pre_value, preferred_element...  13.8 us
  transfers between devices with their start and end apart: 5, of which 5 were waited for; matrix products, arithmetic and copies ran while one was open for 3% of the time, Pallas kernels for 0%

commit v1 on v0

--- a/solution.py
+++ b/solution.py
@@ -116,7 +116,22 @@
     numer = pre_numer + jnp.einsum(
         "skgj,sjkd->skgd", suf_weights, suf_value, preferred_element_type=jnp.float32
     )
-    peak, total, numer = joined((peak, total, numer), "grp", combine_parts)
+    flat = stream_count, kv_local * groups
+    packed = jnp.concatenate(
+        [numer.reshape(stream_count, -1), peak.reshape(flat), total.reshape(flat)], axis=1
+    )
+    everything = lax.all_gather(packed, "grp")
+    width = kv_local * groups * HD
+    heads_local = kv_local * groups
+    all_numer = everything[:, :, :width].reshape(-1, stream_count, kv_local, groups, HD)
+    all_peak = everything[:, :, width : width + heads_local].reshape(
+        -1, stream_count, kv_local, groups
+    )
+    all_total = everything[:, :, width + heads_local :].reshape(-1, stream_count, kv_local, groups)
+    peak = all_peak.max(axis=0)
+    scales = jnp.exp(all_peak - peak[None])
+    total = jnp.sum(all_total * scales, axis=0)
+    numer = jnp.sum(all_numer * scales[..., None], axis=0)
     own_score = (
         jnp.einsum(
             "skgd,skd->skg",
@@ -136,26 +151,30 @@
     partial_out = jnp.dot(attended, w_out, preferred_element_type=jnp.float32)
     share = stream_count // lax.axis_size("tp")
     tp_start = lax.axis_index("tp") * share
-    summed = lax.psum(partial_out, "tp")
-    summed = lax.dynamic_slice_in_dim(summed, tp_start, share, 0)
+    summed = lax.psum_scatter(
+        partial_out.astype(jnp.bfloat16), "tp", scatter_dimension=0, tiled=True
+    )
     own_hidden = lax.dynamic_slice_in_dim(hidden_float, tp_start, share, 0)
-    middle = (own_hidden + summed).astype(jnp.bfloat16)
-    gathered = lax.all_gather(middle, ("pool", "tp"), axis=0, tiled=True)
-    gathered_float = gathered.astype(jnp.float32)
-    ffn_squares = lax.psum(jnp.sum(gathered_float * gathered_float, axis=1), "grp")
+    middle = (own_hidden + summed.astype(jnp.float32)).astype(jnp.bfloat16)
+    middle_float = middle.astype(jnp.float32)
+    ffn_squares = lax.psum(jnp.sum(middle_float * middle_float, axis=1), "grp")
     ffn_inverse = lax.rsqrt(ffn_squares / D + epsilon)
-    normed_ffn = (gathered_float * ffn_inverse[:, None] * ffn_gain).astype(jnp.bfloat16)
+    normed_own = (middle_float * ffn_inverse[:, None] * ffn_gain).astype(jnp.bfloat16)
+    normed_ffn = lax.all_gather(normed_own, ("pool", "tp"), axis=0, tiled=True)
+    hidden_units = w_gate.shape[1]
     part_gate = jnp.dot(normed_ffn, w_gate, preferred_element_type=jnp.float32)
     part_upward = jnp.dot(normed_ffn, w_up, preferred_element_type=jnp.float32)
-    gate, upward = lax.psum((part_gate, part_upward), "grp")
+    both = jnp.concatenate([part_gate, part_upward], axis=1).astype(jnp.bfloat16)
+    reduced = lax.psum_scatter(both, "grp", scatter_dimension=0, tiled=True).astype(jnp.float32)
+    gate = reduced[:, :hidden_units]
+    upward = reduced[:, hidden_units:]
     act = (jax.nn.silu(gate) * upward).astype(jnp.bfloat16)
+    act_all = lax.all_gather(act, "grp", axis=0, tiled=True)
+    down = jnp.dot(act_all, w_down, preferred_element_type=jnp.float32)
     returned = lax.psum_scatter(
-        jnp.dot(act, w_down, preferred_element_type=jnp.float32),
-        ("pool", "tp"),
-        scatter_dimension=0,
-        tiled=True,
-    )
-    return (middle.astype(jnp.float32) + returned).astype(jnp.bfloat16)
+        down.astype(jnp.bfloat16), ("pool", "tp"), scatter_dimension=0, tiled=True
+    )
+    return (middle_float + returned.astype(jnp.float32)).astype(jnp.bfloat16)
 
 
 def solution(mesh):

time: 673 us -> 544 us (0.81)
  waiting for transfers between devices: 466 us -> 346 us
  blocking collectives: 80.4 us -> 67 us
  local copies, waits for them, and re-layouts: 12.8 us -> 19.9 us
    psum x2 -> x0, waiting for transfers between devices: 188 us -> none  [the longest x1 104 us: body(): summed = lax.psum(partial_out, 'tp')]
    all_gather x2, waiting for transfers between devices: 92.6 us -> 135 us  [the longest x1 82 us: body(): normed_ffn = lax.all_gather(normed_own, ('pool', 'tp'), axis=0, tiled=True)]
    reduce_scatter x1 -> x3, waiting for transfers between devices: 186 us -> 211 us  [the longest x1 141 us: body(): lax.psum_scatter(down.astype(jnp.bfloat16), ('pool', 'tp'), scatter_dimen...]
    all_gather x2 -> x1, blocking collectives: 28.3 us -> 14.8 us  [body(): act_all = lax.all_gather(act, 'grp', axis=0, tiled=True)]
    mul x6 -> x2, local copies, waits for them, and re-layouts: 0.75 us -> 7.58 us  [body(): numer = jnp.sum(all_numer * scales[..., None], axis=0)]
  transfers between devices with their start and end apart: 5 -> 5, of which waited for: 5 -> 5; matrix products, arithmetic and copies ran while one was open for 3% -> 0% of each run, Pallas kernels for 0% -> 0%
where the time goes in v1:
time: 544 us; the launch traced here: 543 us
  waiting for transfers between devices  346 us (64%)
  blocking collectives  67 us (12%)
  matrix products  61.2 us (11%)
  other arithmetic  34.9 us (6%)
  local copies, waits for them, and re-layouts  19.9 us (4%)
  between operations  13.5 us (2%)
    reduce_scatter x1, waiting for transfers between devices, body(): lax.psum_scatter(down.astype(jnp.bfloat16), ('pool', 'tp'), scatter_dimen...  141 us
    all_gather x1, waiting for transfers between devices, body(): normed_ffn = lax.all_gather(normed_own, ('pool', 'tp'), axis=0, tiled=True)  82 us
    all_gather x1, waiting for transfers between devices, body(): everything = lax.all_gather(packed, 'grp')  52.9 us
    reduce_scatter x1, waiting for transfers between devices, body(): lax.psum_scatter(partial_out.astype(jnp.bfloat16), 'tp', scatter_dimensio...  40.8 us
    psum x1, blocking collectives, body(): lax.psum((part_query, part_key, part_value), 'grp')  31 us
    reduce_scatter x1, waiting for transfers between devices, body(): lax.psum_scatter(both, 'grp', scatter_dimension=0, tiled=True)  29.3 us
    all_gather x1, blocking collectives, body(): act_all = lax.all_gather(act, 'grp', axis=0, tiled=True)  14.8 us
    dot_general x1, matrix products, body(): jnp.einsum('pskgj,pjkd->pskgd', pre_weights, pre_value, preferred_element...  14.1 us
  transfers between devices with their start and end apart: 5, of which 5 were waited for; matrix products, arithmetic and copies ran while one was open for 0% of the time, Pallas kernels for 0%

profile of v1, /device:TPU:0, one launch (start us, length us, event | category | flops | bytes accessed | tf_op | source)
XLA Modules:
  0.0 542.9 jit_solution(16432499461241207437)
XLA Ops:
  12.9 10.9 %psum.35 = f32[256]{0:T(256)S(1)} all-reduce(f32[256]{0:T(256)S(1)} %multiply_reduce_fusion), channel_id=1, replica_groups=mesh['pool'=4,'grp'=4,'tp'=8] {'grp'}, use_global_device_ids=true, to_apply=%region_1.0 | all-reduce | flops 256 | bytes 2048 | tf_op jit(solution)/shard_map/psum | solution.py:56
  23.8 4.9 fusion.36
  29.7 31.0 %all-reduce.2 = (bf16[256,1024]{1,0:T(8,128)(2,1)S(1)}, bf16[256,128]{1,0:T(8,128)(2,1)S(1)}, bf16[256,128]{1,0:T(8,128)(2,1)S(1)}) all-reduce(f32[256,1024]{1,0:T(8,128)} %fusion.36, f32[256,128]{1,0:T(8,128)S(1)} %fusion.35, f32[256,128]{1,0:T(8,128)S(1)} %fusion.34), channel_id=1, replica_groups=mesh['pool'=4,'grp'=4,'tp'=8] {'grp'}, use_global_device_ids=true, to_apply=%region_2.0 | all-reduce | flops 327680 | bytes 1966080 | tf_op jit(solution)/shard_map/psum | solution.py:62
  61.6 13.1 %bitcast_reduce_fusion = (f32[2,128,8]{1,2,0:T(8,128)S(1)}, f32[2,128,8,4096]{3,1,2,0:T(8,128)}) fusion(bf16[2,4096,128]{2,1,0:T(8,128)(2,1)S(1)} %copy-done, bf16[2,128,8,128]{3,2,1,0:T(8,128)(2,1)S(1)} %bitcast.128), kind=kOutput, calls=%fused_computation.7 | convolution fusion | flops 2164258816 | bytes 36184064 | tf_op jit(solution)/shard_map/pskgd,pjkd->pskgj/dot_general | solution.py:92
  75.7 4.5 fusion.39
  81.1 14.0 %convert_reduce_fusion = f32[2,128,8]{1,2,0:T(8,128)S(1)} fusion(f32[2,128,8]{1,2,0:T(8,128)S(1)} %copy.38, f32[2,128,8,4096]{3,1,2,0:T(8,128)} %get-tuple-element.16), kind=kLoop, calls=%fused_computation.10 | loop fusion | flops 41940992 | bytes 33570816 | tf_op jit(solution)/shard_map/reduce_sum | solution.py:106
  96.7 14.1 %fusion.10 = f32[2,128,1,8,128]{4,1,3,0,2:T(8,128)S(1)} fusion(bf16[2,4096,128]{2,1,0:T(8,128)(2,1)} %param.23, f32[2,128,8]{1,2,0:T(8,128)S(1)} %copy.38, f32[2,128,8,4096]{3,1,2,0:T(8,128)} %get-tuple-element.16), kind=kOutput, calls=%fused_computation.28 | convolution fusion | flops 2172649472 | bytes 36708352 | tf_op jit(solution)/shard_map/pskgj,pjkd->pskgd/dot_general | solution.py:108
  110.8 1.6 copy.39
  112.4 3.0 gather_fusion.3
  115.4 3.7 convolution_add_fusion
  121.2 52.9 %all-gather.6.cloned.1.call-done = f32[1024,1040]{1,0:T(8,128)} async-done(((f32[256,1040]{1,0:T(8,128)}), f32[1024,1040]{1,0:T(8,128)}) %all-gather.6.cloned.1.call-update) | async-done | bytes 4259856 | tf_op jit(solution)/shard_map/all_gather | solution.py:123
  176.8 2.6 mul.163
  179.4 5.0 mul.164
  184.4 4.5 fusion.4
  190.4 4.8 convolution_convert_fusion.1
  196.9 40.8 %reduce-scatter.4.cloned.1.call-done = bf16[32,2048]{1,0:T(8,128)(2,1)} async-done(((bf16[256,2048]{1,0:T(8,128)(2,1)}), bf16[32,2048]{1,0:T(8,128)(2,1)}) %reduce-scatter.4.cloned.1.call-update) | async-done | bytes 131088 | tf_op jit(solution)/shard_map/reduce_scatter | solution.py:154
  238.9 10.4 %psum.39 = f32[32]{0:T(128)S(1)} all-reduce(f32[32]{0:T(128)S(1)} %get-tuple-element.8), channel_id=1, replica_groups=mesh['pool'=4,'grp'=4,'tp'=8] {'grp'}, use_global_device_ids=true, to_apply=%region_18.19 | all-reduce | flops 32 | bytes 256 | tf_op jit(solution)/shard_map/psum | solution.py:160
  250.1 82.0 %all-gather.4.cloned.1.call-done = bf16[1024,2048]{1,0:T(8,128)(2,1)} async-done(((bf16[32,2048]{1,0:T(8,128)(2,1)}), bf16[1024,2048]{1,0:T(8,128)(2,1)}) %all-gather.4.cloned.1.call-update) | async-done | bytes 4194320 | tf_op jit(solution)/shard_map/all_gather | solution.py:163
  332.1 5.0 convolution_convert_fusion.2
  337.1 3.6 convolution_convert_fusion.3
  342.2 29.3 %reduce-scatter.6.cloned.1.call-done = bf16[256,896]{0,1:T(8,128)(2,1)} async-done(((bf16[1024,896]{0,1:T(8,128)(2,1)}), bf16[256,896]{0,1:T(8,128)(2,1)}) %reduce-scatter.6.cloned.1.call-update) | async-done | bytes 458768 | tf_op jit(solution)/shard_map/reduce_scatter | solution.py:168
  372.8 14.8 %all_gather.15 = bf16[1024,448]{0,1:T(8,128)(2,1)S(1)} all-gather(bf16[256,448]{0,1:T(8,128)(2,1)S(1)} %fusion.19), channel_id=1, replica_groups=mesh['pool'=4,'grp'=4,'tp'=8] {'grp'}, dimensions={0}, use_global_device_ids=true | all-gather | bytes 1146880 | tf_op jit(solution)/shard_map/all_gather | solution.py:172
  387.6 6.0 %convolution_convert_fusion = bf16[1024,2048]{1,0:T(8,128)(2,1)} fusion(bf16[1024,448]{0,1:T(8,128)(2,1)S(1)} %all_gather.15, bf16[448,2048]{1,0:T(8,128)(2,1)} %param.31), kind=kOutput, calls=%fused_computation.15 | convolution fusion | flops 1881145344 | bytes 6946816 | tf_op jit(solution)/shard_map/dot_general | solution.py:173
  393.6 141.2 %reduce-scatter.8.cloned.1.call-done = bf16[32,2048]{1,0:T(8,128)(2,1)} async-done(((bf16[1024,2048]{1,0:T(8,128)(2,1)}), bf16[32,2048]{1,0:T(8,128)(2,1)}) %reduce-scatter.8.cloned.1.call-update) | async-done | bytes 131088 | tf_op jit(solution)/shard_map/reduce_scatter | solution.py:174
  (85 shorter events, 25.7 us)
Async XLA Ops:
  6.5 55.1 %copy-start = (bf16[2,4096,128]{2,1,0:T(8,128)(2,1)S(1)}, bf16[2,4096,128]{2,1,0:T(8,128)(2,1)}, u32[]{:S(2)}) copy-start(bf16[2,4096,128]{2,1,0:T(8,128)(2,1)} %param.22) | copy-start | bytes 6291460
  6.5 167.5 %all-gather.6.cloned.1.call-start = ((), (), s32[]{:S(2)}) async-start(), calls=%async_computation.7 | async-start | bytes 5898240 | tf_op jit(solution)/shard_map/all_gather | solution.py:123
  11.3 17.4 %copy-start.2 = (bf16[256,2048]{1,0:T(8,128)(2,1)S(1)}, bf16[256,2048]{1,0:T(8,128)(2,1)}, u32[]{:S(2)}) copy-start(bf16[256,2048]{1,0:T(8,128)(2,1)} %param.16) | copy-start | bytes 3145732
  11.3 17.4 %copy-start.9 = (f32[2048]{0:T(1024)S(1)}, f32[2048]{0:T(1024)}, u32[]{:S(2)}) copy-start(f32[2048]{0:T(1024)} %param.17) | copy-start | bytes 24580
  23.8 4.9 copy-start.7
  23.8 5.4 %copy-start.8 = (bf16[2048,128]{1,0:T(8,128)(2,1)S(1)}, bf16[2048,128]{1,0:T(8,128)(2,1)}, u32[]{:S(2)}) copy-start(bf16[2048,128]{1,0:T(8,128)(2,1)} %param.19) | copy-start | bytes 1572868
  61.6 14.0 %copy-start.5 = (s32[256]{0:T(256)S(1)}, s32[256]{0:T(256)}, u32[]{:S(2)}) copy-start(s32[256]{0:T(256)} %param.27) | copy-start | bytes 3076
  120.6 117.1 %reduce-scatter.4.cloned.1.call-start = ((), (), s32[]{:S(2)}) async-start(), calls=%async_computation.3 | async-start | bytes 1179648 | tf_op jit(solution)/shard_map/reduce_scatter | solution.py:154
  190.4 4.9 copy-start.3
  195.2 54.1 %copy-start.4 = (f32[2048]{0:T(1024)S(1)}, f32[2048]{0:T(1024)}, u32[]{:S(2)}) copy-start(f32[2048]{0:T(1024)} %param.28) | copy-start | bytes 24580
  195.3 136.9 %all-gather.4.cloned.1.call-start = ((), (), s32[]{:S(2)}) async-start(), calls=%async_computation.4 | async-start | bytes 4325376 | tf_op jit(solution)/shard_map/all_gather | solution.py:163
  250.1 121.5 %reduce-scatter.6.cloned.1.call-start = ((), (), s32[]{:S(2)}) async-start(), calls=%async_computation.5 | async-start | bytes 2293760 | tf_op jit(solution)/shard_map/reduce_scatter | solution.py:168
  332.1 5.0 copy-start.6
  342.2 192.6 %reduce-scatter.8.cloned.1.call-start = ((), (), s32[]{:S(2)}) async-start(), calls=%async_computation.6 | async-start | bytes 4325376 | tf_op jit(solution)/shard_map/reduce_scatter | solution.py:174
  387.6 148.8 %copy-start.1 = (bf16[2,4096,128]{2,1,0:T(8,128)(2,1)S(1)}, bf16[2,4096,128]{2,1,0:T(8,128)(2,1)}, u32[]{:S(2)}) copy-start(bf16[2,4096,128]{2,1,0:T(8,128)(2,1)} %param.22) | copy-start | bytes 6291460
Sparse Core Ops, SparseCore 0:
  120.7 53.2 all-gather.5
  195.4 42.2 reduce-scatter.3
  250.2 81.8 all-gather.3
  342.3 29.1 reduce-scatter.5
  393.7 141.0 reduce-scatter.7

commit v2 on v1

--- a/solution.py
+++ b/solution.py
@@ -75,7 +75,8 @@
     pre_value = prefix_values.reshape(prefix_local, pre_length, kv_local, HD)
     suf_key = suffix_keys.reshape(stream_count, suf_length, kv_local, HD)
     suf_value = suffix_values.reshape(stream_count, suf_length, kv_local, HD)
-    local_prefix = prefix_ids - lax.axis_index("pool") * prefix_local
+    pool_index = lax.axis_index("hi") * lax.axis_size("core") + lax.axis_index("core")
+    local_prefix = prefix_ids - pool_index * prefix_local
     per_group = stream_count // prefix_local
     one_hot = (local_prefix[:, None] == jnp.arange(prefix_local, dtype=jnp.int32)[None, :]).astype(
         jnp.int32
@@ -160,45 +161,56 @@
     ffn_squares = lax.psum(jnp.sum(middle_float * middle_float, axis=1), "grp")
     ffn_inverse = lax.rsqrt(ffn_squares / D + epsilon)
     normed_own = (middle_float * ffn_inverse[:, None] * ffn_gain).astype(jnp.bfloat16)
-    normed_ffn = lax.all_gather(normed_own, ("pool", "tp"), axis=0, tiled=True)
-    hidden_units = w_gate.shape[1]
-    part_gate = jnp.dot(normed_ffn, w_gate, preferred_element_type=jnp.float32)
-    part_upward = jnp.dot(normed_ffn, w_up, preferred_element_type=jnp.float32)
+    swap = [(0, 1), (1, 0)]
+    gate_both = jnp.concatenate([w_gate, lax.ppermute(w_gate, "core", swap)], axis=1)
+    up_both = jnp.concatenate([w_up, lax.ppermute(w_up, "core", swap)], axis=1)
+    down_both = jnp.concatenate([w_down, lax.ppermute(w_down, "core", swap)], axis=0)
+    normed_half = lax.all_gather(normed_own, ("hi", "tp"), axis=0, tiled=True)
+    hidden_units = gate_both.shape[1]
+    part_gate = jnp.dot(normed_half, gate_both, preferred_element_type=jnp.float32)
+    part_upward = jnp.dot(normed_half, up_both, preferred_element_type=jnp.float32)
     both = jnp.concatenate([part_gate, part_upward], axis=1).astype(jnp.bfloat16)
     reduced = lax.psum_scatter(both, "grp", scatter_dimension=0, tiled=True).astype(jnp.float32)
     gate = reduced[:, :hidden_units]
     upward = reduced[:, hidden_units:]
     act = (jax.nn.silu(gate) * upward).astype(jnp.bfloat16)
     act_all = lax.all_gather(act, "grp", axis=0, tiled=True)
-    down = jnp.dot(act_all, w_down, preferred_element_type=jnp.float32)
+    down = jnp.dot(act_all, down_both, preferred_element_type=jnp.float32)
     returned = lax.psum_scatter(
-        down.astype(jnp.bfloat16), ("pool", "tp"), scatter_dimension=0, tiled=True
+        down.astype(jnp.bfloat16), ("hi", "tp"), scatter_dimension=0, tiled=True
     )
     return (middle_float + returned.astype(jnp.float32)).astype(jnp.bfloat16)
 
 
 def solution(mesh):
+    pool = ("hi", "core")
+    chip_mesh = jax.sharding.Mesh(
+        mesh.devices.reshape(
+            mesh.shape["pool"] // 2, 2, mesh.shape["grp"], mesh.shape["tp"]
+        ),
+        ("hi", "core", "grp", "tp"),
+    )
     return jax.shard_map(
         body,
-        mesh=mesh,
+        mesh=chip_mesh,
         in_specs=(
-            P("pool", "grp"),
+            P(pool, "grp"),
             P("grp"),
             P("grp", "tp"),
             P("grp", "tp"),
             P("grp", "tp"),
             P("tp", "grp"),
-            P("pool", "grp", "tp"),
-            P("pool", "grp", "tp"),
-            P("pool", "grp", "tp"),
-            P("pool", "grp", "tp"),
-            P("pool"),
-            P("pool"),
+            P(pool, "grp", "tp"),
+            P(pool, "grp", "tp"),
+            P(pool, "grp", "tp"),
+            P(pool, "grp", "tp"),
+            P(pool),
+            P(pool),
             P("grp"),
-            P("grp", ("pool", "tp")),
-            P("grp", ("pool", "tp")),
-            P(("pool", "tp"), "grp"),
+            P("grp", pool + ("tp",)),
+            P("grp", pool + ("tp",)),
+            P(pool + ("tp",), "grp"),
         ),
-        out_specs=P(("pool", "tp"), "grp"),
+        out_specs=P(pool + ("tp",), "grp"),
         check_vma=False,
     )

time: 544 us -> 474 us (0.87)
  waiting for transfers between devices: 346 us -> 274 us
    reduce_scatter x1, waiting for transfers between devices: 141 us -> 81.5 us  [body(): lax.psum_scatter(down.astype(jnp.bfloat16), ('hi', 'tp'), scatter_dimensi...]
    all_gather x1, waiting for transfers between devices: 82 us -> 68 us  [body(): normed_half = lax.all_gather(normed_own, ('hi', 'tp'), axis=0, tiled=True)]
  transfers between devices with their start and end apart: 5 -> 8, of which waited for: 5 -> 6; matrix products, arithmetic and copies ran while one was open for 0% -> 2% of each run, Pallas kernels for 0% -> 0%
where the time goes in v2:
time: 474 us; the launch traced here: 473 us
  waiting for transfers between devices  274 us (58%)
  blocking collectives  66.7 us (14%)
  matrix products  61.2 us (13%)
  other arithmetic  34.8 us (7%)
  local copies, waits for them, and re-layouts  22.2 us (5%)
  between operations  13.5 us (3%)
    reduce_scatter x1, waiting for transfers between devices, body(): lax.psum_scatter(down.astype(jnp.bfloat16), ('hi', 'tp'), scatter_dimensi...  81.5 us
    all_gather x1, waiting for transfers between devices, body(): normed_half = lax.all_gather(normed_own, ('hi', 'tp'), axis=0, tiled=True)  68 us
    all_gather x1, waiting for transfers between devices, body(): everything = lax.all_gather(packed, 'grp')  52.8 us
    reduce_scatter x1, waiting for transfers between devices, body(): lax.psum_scatter(partial_out.astype(jnp.bfloat16), 'tp', scatter_dimensio...  40.8 us
    psum x1, blocking collectives, body(): lax.psum((part_query, part_key, part_value), 'grp')  30.9 us
    reduce_scatter x1, waiting for transfers between devices, body(): lax.psum_scatter(both, 'grp', scatter_dimension=0, tiled=True)  27.2 us
    all_gather x1, blocking collectives, body(): act_all = lax.all_gather(act, 'grp', axis=0, tiled=True)  14.5 us
    dot_general x1, matrix products, body(): jnp.einsum('pskgj,pjkd->pskgd', pre_weights, pre_value, preferred_element...  14.1 us
  transfers between devices with their start and end apart: 8, of which 6 were waited for; matrix products, arithmetic and copies ran while one was open for 2% of the time, Pallas kernels for 0%

profile of v2, /device:TPU:0, one launch (start us, length us, event | category | flops | bytes accessed | tf_op | source)
XLA Modules:
  0.0 473.0 jit_solution(5284992951698860635)
XLA Ops:
  12.8 10.9 %psum.35 = f32[256]{0:T(256)S(1)} all-reduce(f32[256]{0:T(256)S(1)} %multiply_reduce_fusion), channel_id=1, replica_groups=mesh['hi'=2,'core'=2,'grp'=4,'tp'=8] {'grp'}, use_global_device_ids=true, to_apply=%region_1.0 | all-reduce | flops 256 | bytes 2048 | tf_op jit(solution)/shard_map/psum | solution.py:56
  23.7 4.0 fusion.60
  28.7 30.9 %all-reduce.2 = (bf16[256,1024]{1,0:T(8,128)(2,1)}, bf16[256,128]{1,0:T(8,128)(2,1)S(1)}, bf16[256,128]{1,0:T(8,128)(2,1)S(1)}) all-reduce(f32[256,1024]{1,0:T(8,128)S(1)} %fusion.60, f32[256,128]{1,0:T(8,128)S(1)} %fusion.59, f32[256,128]{1,0:T(8,128)S(1)} %fusion.58), channel_id=1, replica_groups=mesh['hi'=2,'core'=2,'grp'=4,'tp'=8] {'grp'}, use_global_device_ids=true, to_apply=%region_2.0 | all-reduce | flops 327680 | bytes 1966080 | tf_op jit(solution)/shard_map/psum | solution.py:62
  61.6 13.1 %bitcast_reduce_fusion = (f32[2,128,8]{1,2,0:T(8,128)S(1)}, f32[2,128,8,4096]{3,1,2,0:T(8,128)}) fusion(bf16[2,4096,128]{2,1,0:T(8,128)(2,1)S(1)} %copy-done, bf16[2,128,8,128]{3,2,1,0:T(8,128)(2,1)S(1)} %bitcast.125), kind=kOutput, calls=%fused_computation.7 | convolution fusion | flops 2164258816 | bytes 36184064 | tf_op jit(solution)/shard_map/pskgd,pjkd->pskgj/dot_general | solution.py:93
  75.7 4.5 fusion.63
  81.0 14.0 %convert_reduce_fusion = f32[2,128,8]{1,2,0:T(8,128)S(1)} fusion(f32[2,128,8]{1,2,0:T(8,128)S(1)} %copy.38, f32[2,128,8,4096]{3,1,2,0:T(8,128)} %get-tuple-element.16), kind=kLoop, calls=%fused_computation.10 | loop fusion | flops 41940992 | bytes 33570816 | tf_op jit(solution)/shard_map/reduce_sum | solution.py:107
  96.7 14.1 %fusion.31 = f32[2,128,1,8,128]{4,1,3,0,2:T(8,128)S(1)} fusion(bf16[2,4096,128]{2,1,0:T(8,128)(2,1)} %param.23, f32[2,128,8]{1,2,0:T(8,128)S(1)} %copy.38, f32[2,128,8,4096]{3,1,2,0:T(8,128)} %get-tuple-element.16), kind=kOutput, calls=%fused_computation.40 | convolution fusion | flops 2172649472 | bytes 36708352 | tf_op jit(solution)/shard_map/pskgj,pjkd->pskgd/dot_general | solution.py:109
  112.3 3.0 gather_fusion.3
  115.3 3.8 convolution_add_fusion
  121.1 52.8 %all-gather.6.cloned.1.call-done = f32[1024,1040]{1,0:T(8,128)} async-done(((f32[256,1040]{1,0:T(8,128)}), f32[1024,1040]{1,0:T(8,128)}) %all-gather.6.cloned.1.call-update) | async-done | bytes 4259856 | tf_op jit(solution)/shard_map/all_gather | solution.py:124
  176.6 2.6 mul.167
  179.3 5.0 %mul.168 = f32[4,256,1024]{2,1,0:T(8,128)} reshape(f32[4,256,8,128]{3,2,1,0:T(8,128)} %mul.167) | data formatting | bytes 8388608 | tf_op jit(solution)/shard_map/mul | solution.py:135
  184.2 4.5 fusion.4
  190.3 4.8 %convolution_convert_fusion = bf16[256,2048]{1,0:T(8,128)(2,1)} fusion(bf16[1024,2048]{1,0:T(8,128)(2,1)} %param.21, f32[32,8,8,128]{3,2,1,0:T(8,128)S(1)} %bitcast.128, f32[32,8,8,128]{3,2,1,0:T(8,128)S(1)} %bitcast.126, f32[256,1024]{1,0:T(8,128)S(1)} %fusion.4, f32[32,8,8,128]{3,2,1,0:T(8,128)S(1)} %bitcast.127), kind=kOutput, calls=%fused_computation.28 | convolution fusion | flops 1075314688 | bytes 9437184 | tf_op jit(solution)/shard_map/dot_general | solution.py:152
  196.8 40.8 %reduce-scatter.4.cloned.1.call-done = bf16[32,2048]{1,0:T(8,128)(2,1)} async-done(((bf16[256,2048]{1,0:T(8,128)(2,1)}), bf16[32,2048]{1,0:T(8,128)(2,1)}) %reduce-scatter.4.cloned.1.call-update) | async-done | bytes 131088 | tf_op jit(solution)/shard_map/reduce_scatter | solution.py:155
  238.7 10.4 %psum.39 = f32[32]{0:T(128)S(1)} all-reduce(f32[32]{0:T(128)S(1)} %get-tuple-element.8), channel_id=1, replica_groups=mesh['hi'=2,'core'=2,'grp'=4,'tp'=8] {'grp'}, use_global_device_ids=true, to_apply=%region_18.19 | all-reduce | flops 32 | bytes 256 | tf_op jit(solution)/shard_map/psum | solution.py:161
  250.6 3.5 collective-permute-done.1
  255.3 68.0 %all-gather.4.cloned.1.call-done = bf16[512,2048]{1,0:T(8,128)(2,1)} async-done(((bf16[32,2048]{1,0:T(8,128)(2,1)}), bf16[512,2048]{1,0:T(8,128)(2,1)}) %all-gather.4.cloned.1.call-update) | async-done | bytes 2097168 | tf_op jit(solution)/shard_map/all_gather | solution.py:168
  323.3 5.2 %fusion.24 = bf16[512,896]{1,0:T(8,128)(2,1)S(1)} fusion(bf16[512,2048]{1,0:T(8,128)(2,1)} %all-gather.4.cloned.1.call-done, bf16[2048,448]{0,1:T(8,128)(2,1)} %copy-done.7, bf16[2048,448]{0,1:T(8,128)(2,1)} %param.30), kind=kOutput, calls=%fused_computation.35 | convolution fusion | flops 1886846976 | bytes 6684672 | tf_op jit(solution)/shard_map/dot_general | solution.py:171
  328.5 4.4 fusion.27
  334.5 27.2 %reduce-scatter.6.cloned.1.call-done = bf16[128,1792]{1,0:T(8,128)(2,1)} async-done(((bf16[512,1792]{1,0:T(8,128)(2,1)}), bf16[128,1792]{1,0:T(8,128)(2,1)}) %reduce-scatter.6.cloned.1.call-update) | async-done | bytes 458768 | tf_op jit(solution)/shard_map/reduce_scatter | solution.py:173
  362.9 14.5 %all_gather.15 = bf16[512,896]{1,0:T(8,128)(2,1)S(1)} all-gather(bf16[128,896]{1,0:T(8,128)(2,1)S(1)} %fusion.40), channel_id=1, replica_groups=mesh['hi'=2,'core'=2,'grp'=4,'tp'=8] {'grp'}, dimensions={0}, use_global_device_ids=true | all-gather | bytes 1146880 | tf_op jit(solution)/shard_map/all_gather | solution.py:177
  377.5 5.9 %fusion.17 = bf16[512,2048]{1,0:T(8,128)(2,1)} fusion(bf16[512,896]{1,0:T(8,128)(2,1)S(1)} %all_gather.15, bf16[448,2048]{1,0:T(8,128)(2,1)} %collective-permute-done.2, bf16[448,2048]{1,0:T(8,128)(2,1)} %param.31), kind=kOutput, calls=%fused_computation.27 | convolution fusion | flops 1887436800 | bytes 6684672 | tf_op jit(solution)/shard_map/dot_general | solution.py:178
  383.4 81.5 %reduce-scatter.8.cloned.1.call-done = bf16[32,2048]{1,0:T(8,128)(2,1)} async-done(((bf16[512,2048]{1,0:T(8,128)(2,1)}), bf16[32,2048]{1,0:T(8,128)(2,1)}) %reduce-scatter.8.cloned.1.call-update) | async-done | bytes 131088 | tf_op jit(solution)/shard_map/reduce_scatter | solution.py:179
  (93 shorter events, 30.2 us)
Async XLA Ops:
  6.5 55.0 %copy-start = (bf16[2,4096,128]{2,1,0:T(8,128)(2,1)S(1)}, bf16[2,4096,128]{2,1,0:T(8,128)(2,1)}, u32[]{:S(2)}) copy-start(bf16[2,4096,128]{2,1,0:T(8,128)(2,1)} %param.22) | copy-start | bytes 6291460
  6.5 167.4 %all-gather.6.cloned.1.call-start = ((), (), s32[]{:S(2)}) async-start(), calls=%async_computation.7 | async-start | bytes 5898240 | tf_op jit(solution)/shard_map/all_gather | solution.py:124
  23.7 4.0 copy-start.2
  23.7 4.0 copy-start.8
  23.7 4.0 copy-start.10
  23.7 4.5 copy-start.9
  61.6 14.0 %copy-start.5 = (s32[256]{0:T(256)S(1)}, s32[256]{0:T(256)}, u32[]{:S(2)}) copy-start(s32[256]{0:T(256)} %param.27) | copy-start | bytes 3076
  120.6 117.0 %reduce-scatter.4.cloned.1.call-start = ((), (), s32[]{:S(2)}) async-start(), calls=%async_computation.3 | async-start | bytes 1179648 | tf_op jit(solution)/shard_map/reduce_scatter | solution.py:155
  190.3 4.9 %copy-start.3 = (bf16[256,2048]{1,0:T(8,128)(2,1)S(1)}, bf16[256,2048]{1,0:T(8,128)(2,1)}, u32[]{:S(2)}) copy-start(bf16[256,2048]{1,0:T(8,128)(2,1)} %param.16) | copy-start | bytes 3145732
  195.1 54.1 %copy-start.4 = (f32[2048]{0:T(1024)S(1)}, f32[2048]{0:T(1024)}, u32[]{:S(2)}) copy-start(f32[2048]{0:T(1024)} %param.28) | copy-start | bytes 24580
  195.1 128.2 %all-gather.4.cloned.1.call-start = ((), (), s32[]{:S(2)}) async-start(), calls=%async_computation.4 | async-start | bytes 2228224 | tf_op jit(solution)/shard_map/all_gather | solution.py:168
  249.9 111.8 %reduce-scatter.6.cloned.1.call-start = ((), (), s32[]{:S(2)}) async-start(), calls=%async_computation.5 | async-start | bytes 2293760 | tf_op jit(solution)/shard_map/reduce_scatter | solution.py:173
  250.0 4.1 collective-permute-start.1
  250.1 78.4 %collective-permute-start = (bf16[2048,448]{0,1:T(8,128)(2,1)}, bf16[2048,448]{0,1:T(8,128)(2,1)}, u32[]{:S(2)}, u32[]{:S(2)}) collective-permute-start(bf16[2048,448]{0,1:T(8,128)(2,1)} %param.29), channel_id=1, source_target_pairs={{0,32},{32,0},{1,33},{33,1},{2,34},{34,2},{3,35},{35,3},{4,36},{36... | collective-permute-start | bytes 5505032 | tf_op jit(solution)/shard_map/ppermute | solution.py:165
  254.1 1.3 copy-start.7
  323.3 5.2 %copy-start.6 = (bf16[512,2048]{1,0:T(8,128)(2,1)S(1)}, bf16[512,2048]{1,0:T(8,128)(2,1)}, u32[]{:S(2)}) copy-start(bf16[512,2048]{1,0:T(8,128)(2,1)} %all-gather.4.cloned.1.call-done) | copy-start | bytes 6291460
  334.4 130.5 %reduce-scatter.8.cloned.1.call-start = ((), (), s32[]{:S(2)}) async-start(), calls=%async_computation.6 | async-start | bytes 2228224 | tf_op jit(solution)/shard_map/reduce_scatter | solution.py:179
  334.4 43.1 %collective-permute-start.2 = (bf16[448,2048]{1,0:T(8,128)(2,1)}, bf16[448,2048]{1,0:T(8,128)(2,1)}, u32[]{:S(2)}, u32[]{:S(2)}) collective-permute-start(bf16[448,2048]{1,0:T(8,128)(2,1)} %param.31), channel_id=1, source_target_pairs={{0,32},{32,0},{1,33},{33,1},{2,34},{34,2},{3,35},{35,3},{4,36},{36... | collective-permute-start | bytes 5505032 | tf_op jit(solution)/shard_map/ppermute | solution.py:167
  377.5 89.0 %copy-start.1 = (bf16[2,4096,128]{2,1,0:T(8,128)(2,1)S(1)}, bf16[2,4096,128]{2,1,0:T(8,128)(2,1)}, u32[]{:S(2)}) copy-start(bf16[2,4096,128]{2,1,0:T(8,128)(2,1)} %param.22) | copy-start | bytes 6291460
Sparse Core Ops, SparseCore 0:
  120.7 53.2 all-gather.5
  195.2 42.2 reduce-scatter.3
  250.1 73.1 all-gather.3
  334.5 27.2 reduce-scatter.5
  383.5 81.2 reduce-scatter.7

commit v3 on v2

--- a/solution.py
+++ b/solution.py
@@ -100,39 +100,6 @@
         jnp.einsum("skgd,sjkd->skgj", heads, suf_key, preferred_element_type=jnp.float32) * factor
     )
     suf_scores = jnp.where(valid, suf_scores, -1e30)
-    peak = jnp.maximum(pre_peak, suf_scores.max(axis=3))
-    peak_grouped = peak[group_order].reshape(prefix_local, per_group, kv_local, groups)
-    pre_weights = jnp.exp(pre_scores - peak_grouped[..., None]).astype(jnp.bfloat16)
-    pre_total = (
-        pre_weights.astype(jnp.float32).sum(axis=4).reshape(stream_count, kv_local, groups)[target]
-    )
-    pre_numer = jnp.einsum(
-        "pskgj,pjkd->pskgd", pre_weights, pre_value, preferred_element_type=jnp.float32
-    )
-    pre_numer = pre_numer.reshape(stream_count, kv_local, groups, HD)[target]
-    suf_weights = jnp.where(valid, jnp.exp(suf_scores - peak[:, :, :, None]), 0.0).astype(
-        jnp.bfloat16
-    )
-    total = pre_total + suf_weights.astype(jnp.float32).sum(axis=3)
-    numer = pre_numer + jnp.einsum(
-        "skgj,sjkd->skgd", suf_weights, suf_value, preferred_element_type=jnp.float32
-    )
-    flat = stream_count, kv_local * groups
-    packed = jnp.concatenate(
-        [numer.reshape(stream_count, -1), peak.reshape(flat), total.reshape(flat)], axis=1
-    )
-    everything = lax.all_gather(packed, "grp")
-    width = kv_local * groups * HD
-    heads_local = kv_local * groups
-    all_numer = everything[:, :, :width].reshape(-1, stream_count, kv_local, groups, HD)
-    all_peak = everything[:, :, width : width + heads_local].reshape(
-        -1, stream_count, kv_local, groups
-    )
-    all_total = everything[:, :, width + heads_local :].reshape(-1, stream_count, kv_local, groups)
-    peak = all_peak.max(axis=0)
-    scales = jnp.exp(all_peak - peak[None])
-    total = jnp.sum(all_total * scales, axis=0)
-    numer = jnp.sum(all_numer * scales[..., None], axis=0)
     own_score = (
         jnp.einsum(
             "skgd,skd->skg",
@@ -142,13 +109,41 @@
         )
         * factor
     )
-    new_peak = jnp.maximum(peak, own_score)
-    rescale = jnp.exp(peak - new_peak)
-    own_weight = jnp.exp(own_score - new_peak).astype(jnp.bfloat16).astype(jnp.float32)
-    total = total * rescale + own_weight
-    own_value = value_new.reshape(stream_count, kv_local, 1, HD).astype(jnp.float32)
-    numer = numer * rescale[..., None] + own_weight[..., None] * own_value
-    attended = (numer / total[..., None]).reshape(stream_count, q_local * HD).astype(jnp.bfloat16)
+    peak = lax.pmax(jnp.maximum(jnp.maximum(pre_peak, suf_scores.max(axis=3)), own_score), "grp")
+    peak_grouped = peak[group_order].reshape(prefix_local, per_group, kv_local, groups)
+    pre_weights = jnp.exp(pre_scores - peak_grouped[..., None]).astype(jnp.bfloat16)
+    unit = jnp.zeros((HD,), pre_value.dtype).at[0].set(1)
+    pre_value_ext = jnp.concatenate(
+        [pre_value, jnp.broadcast_to(unit, pre_value.shape)], axis=3
+    )
+    pre_both = jnp.einsum(
+        "pskgj,pjkd->pskgd", pre_weights, pre_value_ext, preferred_element_type=jnp.float32
+    )
+    pre_both = pre_both.reshape(stream_count, kv_local, groups, 2 * HD)[target]
+    suf_weights = jnp.where(valid, jnp.exp(suf_scores - peak[:, :, :, None]), 0.0).astype(
+        jnp.bfloat16
+    )
+    total = pre_both[..., HD] + suf_weights.astype(jnp.float32).sum(axis=3)
+    numer = pre_both[..., :HD] + jnp.einsum(
+        "skgj,sjkd->skgd", suf_weights, suf_value, preferred_element_type=jnp.float32
+    )
+    flat = stream_count, kv_local * groups
+    packed = jnp.concatenate([numer.reshape(stream_count, -1), total.reshape(flat)], axis=1)
+    reduced = lax.psum_scatter(packed, "grp", scatter_dimension=0, tiled=True)
+    quarter = reduced.shape[0]
+    q_start = lax.axis_index("grp") * quarter
+    width = kv_local * groups * HD
+    numer = reduced[:, :width].reshape(quarter, kv_local, groups, HD)
+    total = reduced[:, width:].reshape(quarter, kv_local, groups)
+    own_score = lax.dynamic_slice_in_dim(own_score, q_start, quarter, 0)
+    own_peak = lax.dynamic_slice_in_dim(peak, q_start, quarter, 0)
+    own_weight = jnp.exp(own_score - own_peak).astype(jnp.bfloat16).astype(jnp.float32)
+    total = total + own_weight
+    own_value = lax.dynamic_slice_in_dim(value_new, q_start, quarter, 0)
+    own_value = own_value.reshape(quarter, kv_local, 1, HD).astype(jnp.float32)
+    numer = numer + own_weight[..., None] * own_value
+    attended = (numer / total[..., None]).reshape(quarter, q_local * HD).astype(jnp.bfloat16)
+    attended = lax.all_gather(attended, "grp", axis=0, tiled=True)
     partial_out = jnp.dot(attended, w_out, preferred_element_type=jnp.float32)
     share = stream_count // lax.axis_size("tp")
     tp_start = lax.axis_index("tp") * share

time: 474 us -> 453 us (0.956)
  blocking collectives: 66.7 us -> 96.7 us
  waiting for transfers between devices: 274 us -> 245 us
  other arithmetic: 34.8 us -> 16.3 us
    all_gather x1 -> x0, waiting for transfers between devices: 52.8 us -> none  [body(): everything = lax.all_gather(packed, 'grp')]
    reduce_scatter x0 -> x1, waiting for transfers between devices: none -> 24.8 us  [body(): reduced = lax.psum_scatter(packed, 'grp', scatter_dimension=0, tiled=True)]
    reduce_sum x4 -> x1, other arithmetic: 20.8 us -> 0.72 us  [body(): total = pre_both[..., HD] + suf_weights.astype(jnp.float32).sum(axis=3)]
    pmax x0 -> x1, blocking collectives: none -> 17.3 us  [body(): lax.pmax(jnp.maximum(jnp.maximum(pre_peak, suf_scores.max(axis=3)), own_s...]
    all_gather x0 -> x1, blocking collectives: none -> 12.8 us  [body(): attended = lax.all_gather(attended, 'grp', axis=0, tiled=True)]
    mul x3 -> x0, local copies, waits for them, and re-layouts: 7.91 us -> none  [the longest x2 7.58 us: body(): numer = jnp.sum(all_numer * scales[..., None], axis=0)]
where the time goes in v3:
time: 453 us; the launch traced here: 452 us
  waiting for transfers between devices  245 us (54%)
  blocking collectives  96.7 us (21%)
  matrix products  61.6 us (14%)
  local copies, waits for them, and re-layouts  18.2 us (4%)
  other arithmetic  16.3 us (4%)
  between operations  13.5 us (3%)
    reduce_scatter x1, waiting for transfers between devices, body(): lax.psum_scatter(down.astype(jnp.bfloat16), ('hi', 'tp'), scatter_dimensi...  81.5 us
    all_gather x1, waiting for transfers between devices, body(): normed_half = lax.all_gather(normed_own, ('hi', 'tp'), axis=0, tiled=True)  67.8 us
    reduce_scatter x1, waiting for transfers between devices, body(): lax.psum_scatter(partial_out.astype(jnp.bfloat16), 'tp', scatter_dimensio...  40 us
    psum x1, blocking collectives, body(): lax.psum((part_query, part_key, part_value), 'grp')  30.7 us
    reduce_scatter x1, waiting for transfers between devices, body(): lax.psum_scatter(both, 'grp', scatter_dimension=0, tiled=True)  27.2 us
    reduce_scatter x1, waiting for transfers between devices, body(): reduced = lax.psum_scatter(packed, 'grp', scatter_dimension=0, tiled=True)  24.8 us
    pmax x1, blocking collectives, body(): lax.pmax(jnp.maximum(jnp.maximum(pre_peak, suf_scores.max(axis=3)), own_s...  17.3 us
    dot_general x1, matrix products, body(): jnp.einsum('pskgj,pjkd->pskgd', pre_weights, pre_value_ext, preferred_ele...  15.1 us
  transfers between devices with their start and end apart: 8, of which 6 were waited for; matrix products, arithmetic and copies ran while one was open for 2% of the time, Pallas kernels for 0%

profile of v3, /device:TPU:0, one launch (start us, length us, event | category | flops | bytes accessed | tf_op | source)
XLA Modules:
  0.0 451.9 jit_solution(5520927758768703236)
XLA Ops:
  12.8 10.9 %psum.35 = f32[256]{0:T(256)S(1)} all-reduce(f32[256]{0:T(256)S(1)} %multiply_reduce_fusion), channel_id=1, replica_groups=mesh['hi'=2,'core'=2,'grp'=4,'tp'=8] {'grp'}, use_global_device_ids=true, to_apply=%region_1.0 | all-reduce | flops 256 | bytes 2048 | tf_op jit(solution)/shard_map/psum | solution.py:56
  23.7 3.9 fusion.60
  29.2 30.7 %all-reduce.2 = (bf16[256,1024]{1,0:T(8,128)(2,1)}, bf16[256,128]{1,0:T(8,128)(2,1)S(1)}, bf16[256,128]{1,0:T(8,128)(2,1)S(1)}) all-reduce(f32[256,1024]{1,0:T(8,128)S(1)} %fusion.60, f32[256,128]{1,0:T(8,128)S(1)} %fusion.59, f32[256,128]{1,0:T(8,128)S(1)} %fusion.58), channel_id=1, replica_groups=mesh['hi'=2,'core'=2,'grp'=4,'tp'=8] {'grp'}, use_global_device_ids=true, to_apply=%region_2.0 | all-reduce | flops 327680 | bytes 1966080 | tf_op jit(solution)/shard_map/psum | solution.py:62
  61.9 13.1 %bitcast_reduce_fusion = (f32[2,128,8]{1,2,0:T(8,128)S(1)}, f32[2,128,8,4096]{3,1,2,0:T(8,128)}) fusion(bf16[2,4096,128]{2,1,0:T(8,128)(2,1)S(1)} %copy-done, bf16[2,128,8,128]{3,2,1,0:T(8,128)(2,1)S(1)} %bitcast.133), kind=kOutput, calls=%fused_computation.6 | convolution fusion | flops 2164258816 | bytes 36184064 | tf_op jit(solution)/shard_map/pskgd,pjkd->pskgj/dot_general | solution.py:93
  76.4 4.5 %fusion.62 = (f32[256,8]{1,0:T(8,128)S(1)}, f32[256,8,64]{2,1,0:T(8,128)S(1)}) fusion(bf16[256,8,128]{2,1,0:T(8,128)(2,1)S(1)} %bitcast.130, bf16[256,64,128]{2,1,0:T(8,128)(2,1)} %param.26, pred[256,64]{1,0:T(8,128)(4,1)S(1)} %broadcast_compare_fusion), kind=kOutput, calls=%fused_computation.102 | convolution fusion | flops 33945600 | bytes 5267456 | tf_op jit(solution)/shard_map/skgd,sjkd->skgj/dot_general | solution.py:100
  81.0 17.3 %pmax.7 = f32[256,1,8]{2,0,1:T(8,128)S(1)} all-reduce(f32[256,1,8]{2,0,1:T(8,128)S(1)} %get-tuple-element.25), channel_id=1, replica_groups=mesh['hi'=2,'core'=2,'grp'=4,'tp'=8] {'grp'}, use_global_device_ids=true, to_apply=%region_10.11 | all-reduce | flops 2048 | bytes 16384 | tf_op jit(solution)/shard_map/pmax | solution.py:112
  99.1 15.1 %fusion.26 = f32[2,128,1,8,256]{4,1,3,0,2:T(8,128)} fusion(f32[2,128,8,4096]{3,1,2,0:T(8,128)} %get-tuple-element.27, f32[2,128,8]{1,2,0:T(8,128)S(1)} %copy.26, bf16[2,4096,1,128]{3,1,0,2:T(8,128)(2,1)} %bitcast.140, bf16[256]{0:T(256)(128)(2,1)S(1)} %pad.13.clone), kind=kOutput, calls=%fused_computation.35 | convolution fusion | flops 4328521728 | bytes 37757440 | tf_op jit(solution)/shard_map/pskgj,pjkd->pskgd/dot_general | solution.py:119
  114.2 4.2 copy.27
  118.4 3.6 gather_fusion.3
  124.2 3.5 fusion.35
  130.8 24.8 %reduce-scatter.5.cloned.1.call-done = f32[64,1032]{1,0:T(8,128)} async-done(((f32[256,1032]{1,0:T(8,128)}), f32[64,1032]{1,0:T(8,128)}) %reduce-scatter.5.cloned.1.call-update) | async-done | bytes 264208 | tf_op jit(solution)/shard_map/reduce_scatter | solution.py:132
  157.6 12.8 %all_gather.9 = bf16[256,1024]{1,0:T(8,128)(2,1)S(1)} all-gather(bf16[64,1024]{1,0:T(8,128)(2,1)S(1)} %fusion.43), channel_id=1, replica_groups=mesh['hi'=2,'core'=2,'grp'=4,'tp'=8] {'grp'}, dimensions={0}, use_global_device_ids=true | all-gather | bytes 655360 | tf_op jit(solution)/shard_map/all_gather | solution.py:146
  170.3 4.5 convolution_convert_fusion
  175.0 1.6 convert_element_type.75
  176.6 40.0 %reduce-scatter.7.cloned.1.call-done = bf16[32,2048]{1,0:T(8,128)(2,1)} async-done(((bf16[256,2048]{1,0:T(8,128)(2,1)}), bf16[32,2048]{1,0:T(8,128)(2,1)}) %reduce-scatter.7.cloned.1.call-update) | async-done | bytes 131088 | tf_op jit(solution)/shard_map/reduce_scatter | solution.py:150
  217.8 10.5 %psum.39 = f32[32]{0:T(128)S(1)} all-reduce(f32[32]{0:T(128)S(1)} %get-tuple-element.20), channel_id=1, replica_groups=mesh['hi'=2,'core'=2,'grp'=4,'tp'=8] {'grp'}, use_global_device_ids=true, to_apply=%region_16.17 | all-reduce | flops 32 | bytes 256 | tf_op jit(solution)/shard_map/psum | solution.py:156
  229.7 3.5 collective-permute-done.1
  234.4 67.8 %all-gather.2.cloned.1.call-done = bf16[512,2048]{1,0:T(8,128)(2,1)} async-done(((bf16[32,2048]{1,0:T(8,128)(2,1)}), bf16[512,2048]{1,0:T(8,128)(2,1)}) %all-gather.2.cloned.1.call-update) | async-done | bytes 2097168 | tf_op jit(solution)/shard_map/all_gather | solution.py:163
  302.2 5.2 %fusion.29 = bf16[512,896]{1,0:T(8,128)(2,1)S(1)} fusion(bf16[512,2048]{1,0:T(8,128)(2,1)} %all-gather.2.cloned.1.call-done, bf16[2048,448]{0,1:T(8,128)(2,1)} %copy-done.8, bf16[2048,448]{0,1:T(8,128)(2,1)} %param.32), kind=kOutput, calls=%fused_computation.36 | convolution fusion | flops 1886846976 | bytes 6684672 | tf_op jit(solution)/shard_map/dot_general | solution.py:166
  307.4 4.4 fusion.32
  313.4 27.2 %reduce-scatter.9.cloned.1.call-done = bf16[128,1792]{1,0:T(8,128)(2,1)} async-done(((bf16[512,1792]{1,0:T(8,128)(2,1)}), bf16[128,1792]{1,0:T(8,128)(2,1)}) %reduce-scatter.9.cloned.1.call-update) | async-done | bytes 458768 | tf_op jit(solution)/shard_map/reduce_scatter | solution.py:168
  341.8 14.6 %all_gather.11 = bf16[512,896]{1,0:T(8,128)(2,1)S(1)} all-gather(bf16[128,896]{1,0:T(8,128)(2,1)S(1)} %fusion.38), channel_id=1, replica_groups=mesh['hi'=2,'core'=2,'grp'=4,'tp'=8] {'grp'}, dimensions={0}, use_global_device_ids=true | all-gather | bytes 1146880 | tf_op jit(solution)/shard_map/all_gather | solution.py:172
  356.4 5.9 %fusion.20 = bf16[512,2048]{1,0:T(8,128)(2,1)} fusion(bf16[512,896]{1,0:T(8,128)(2,1)S(1)} %all_gather.11, bf16[448,2048]{1,0:T(8,128)(2,1)} %collective-permute-done.2, bf16[448,2048]{1,0:T(8,128)(2,1)} %param.33), kind=kOutput, calls=%fused_computation.27 | convolution fusion | flops 1887436800 | bytes 6684672 | tf_op jit(solution)/shard_map/dot_general | solution.py:173
  362.3 81.5 %reduce-scatter.11.cloned.1.call-done = bf16[32,2048]{1,0:T(8,128)(2,1)} async-done(((bf16[512,2048]{1,0:T(8,128)(2,1)}), bf16[32,2048]{1,0:T(8,128)(2,1)}) %reduce-scatter.11.cloned.1.call-update) | async-done | bytes 131088 | tf_op jit(solution)/shard_map/reduce_scatter | solution.py:174
  (89 shorter events, 27.4 us)
Async XLA Ops:
  6.5 55.3 %copy-start = (bf16[2,4096,128]{2,1,0:T(8,128)(2,1)S(1)}, bf16[2,4096,128]{2,1,0:T(8,128)(2,1)}, u32[]{:S(2)}) copy-start(bf16[2,4096,128]{2,1,0:T(8,128)(2,1)} %param.24) | copy-start | bytes 6291460
  6.5 149.1 %reduce-scatter.5.cloned.1.call-start = ((), (), s32[]{:S(2)}) async-start(), calls=%async_computation.4 | async-start | bytes 1474560 | tf_op jit(solution)/shard_map/reduce_scatter | solution.py:132
  23.7 4.0 copy-start.3
  23.7 4.0 copy-start.9
  23.7 4.0 copy-start.11
  27.7 1.0 copy-start.10
  75.0 1.3 copy-start.6
  80.9 18.1 %copy-start.12 = (bf16[128]{0:T(256)(128)(2,1)S(1)}, bf16[128]{0:T(256)(128)(2,1)}, u32[]{:S(2)}) copy-start(bf16[128]{0:T(256)(128)(2,1)} %constant.73.clone.1) | copy-start | bytes 772
  122.0 2.2 copy-start.2
  130.6 86.0 %reduce-scatter.7.cloned.1.call-start = ((), (), s32[]{:S(2)}) async-start(), calls=%async_computation.5 | async-start | bytes 1179648 | tf_op jit(solution)/shard_map/reduce_scatter | solution.py:150
  170.3 4.6 %copy-start.4 = (bf16[256,2048]{1,0:T(8,128)(2,1)S(1)}, bf16[256,2048]{1,0:T(8,128)(2,1)}, u32[]{:S(2)}) copy-start(bf16[256,2048]{1,0:T(8,128)(2,1)} %param.18) | copy-start | bytes 3145732
  174.9 53.4 %copy-start.5 = (f32[2048]{0:T(1024)S(1)}, f32[2048]{0:T(1024)}, u32[]{:S(2)}) copy-start(f32[2048]{0:T(1024)} %param.30) | copy-start | bytes 24580
  174.9 127.3 %all-gather.2.cloned.1.call-start = ((), (), s32[]{:S(2)}) async-start(), calls=%async_computation.6 | async-start | bytes 2228224 | tf_op jit(solution)/shard_map/all_gather | solution.py:163
  229.1 111.6 %reduce-scatter.9.cloned.1.call-start = ((), (), s32[]{:S(2)}) async-start(), calls=%async_computation.7 | async-start | bytes 2293760 | tf_op jit(solution)/shard_map/reduce_scatter | solution.py:168
  229.1 4.1 collective-permute-start.1
  229.2 78.2 %collective-permute-start = (bf16[2048,448]{0,1:T(8,128)(2,1)}, bf16[2048,448]{0,1:T(8,128)(2,1)}, u32[]{:S(2)}, u32[]{:S(2)}) collective-permute-start(bf16[2048,448]{0,1:T(8,128)(2,1)} %param.31), channel_id=1, source_target_pairs={{0,32},{32,0},{1,33},{33,1},{2,34},{34,2},{3,35},{35,3},{4,36},{36... | collective-permute-start | bytes 5505032 | tf_op jit(solution)/shard_map/ppermute | solution.py:160
  233.2 1.3 copy-start.8
  302.2 5.2 %copy-start.7 = (bf16[512,2048]{1,0:T(8,128)(2,1)S(1)}, bf16[512,2048]{1,0:T(8,128)(2,1)}, u32[]{:S(2)}) copy-start(bf16[512,2048]{1,0:T(8,128)(2,1)} %all-gather.2.cloned.1.call-done) | copy-start | bytes 6291460
  313.3 130.5 %reduce-scatter.11.cloned.1.call-start = ((), (), s32[]{:S(2)}) async-start(), calls=%async_computation.8 | async-start | bytes 2228224 | tf_op jit(solution)/shard_map/reduce_scatter | solution.py:174
  313.3 43.1 %collective-permute-start.2 = (bf16[448,2048]{1,0:T(8,128)(2,1)}, bf16[448,2048]{1,0:T(8,128)(2,1)}, u32[]{:S(2)}, u32[]{:S(2)}) collective-permute-start(bf16[448,2048]{1,0:T(8,128)(2,1)} %param.33), channel_id=1, source_target_pairs={{0,32},{32,0},{1,33},{33,1},{2,34},{34,2},{3,35},{35,3},{4,36},{36... | collective-permute-start | bytes 5505032 | tf_op jit(solution)/shard_map/ppermute | solution.py:162
  356.4 89.0 %copy-start.1 = (bf16[2,4096,128]{2,1,0:T(8,128)(2,1)S(1)}, bf16[2,4096,128]{2,1,0:T(8,128)(2,1)}, u32[]{:S(2)}) copy-start(bf16[2,4096,128]{2,1,0:T(8,128)(2,1)} %param.24) | copy-start | bytes 6291460
Sparse Core Ops, SparseCore 0:
  130.7 24.8 reduce-scatter.4
  175.0 41.5 reduce-scatter.6
  229.2 72.9 all-gather.1
  313.4 27.2 reduce-scatter.8
  362.4 81.2 reduce-scatter.10

commit v4 on v3

--- a/solution.py
+++ b/solution.py
@@ -7,6 +7,7 @@
 
 D = 8192
 HD = 128
+TP = ("z", "xlo")
 
 
 epsilon = 1e-05
@@ -145,10 +146,10 @@
     attended = (numer / total[..., None]).reshape(quarter, q_local * HD).astype(jnp.bfloat16)
     attended = lax.all_gather(attended, "grp", axis=0, tiled=True)
     partial_out = jnp.dot(attended, w_out, preferred_element_type=jnp.float32)
-    share = stream_count // lax.axis_size("tp")
-    tp_start = lax.axis_index("tp") * share
+    share = stream_count // (lax.axis_size("z") * lax.axis_size("xlo"))
+    tp_start = (lax.axis_index("z") * lax.axis_size("xlo") + lax.axis_index("xlo")) * share
     summed = lax.psum_scatter(
-        partial_out.astype(jnp.bfloat16), "tp", scatter_dimension=0, tiled=True
+        partial_out.astype(jnp.bfloat16), TP, scatter_dimension=0, tiled=True
     )
     own_hidden = lax.dynamic_slice_in_dim(hidden_float, tp_start, share, 0)
     middle = (own_hidden + summed.astype(jnp.float32)).astype(jnp.bfloat16)
@@ -160,7 +161,8 @@
     gate_both = jnp.concatenate([w_gate, lax.ppermute(w_gate, "core", swap)], axis=1)
     up_both = jnp.concatenate([w_up, lax.ppermute(w_up, "core", swap)], axis=1)
     down_both = jnp.concatenate([w_down, lax.ppermute(w_down, "core", swap)], axis=0)
-    normed_half = lax.all_gather(normed_own, ("hi", "tp"), axis=0, tiled=True)
+    normed_row = lax.all_gather(normed_own, ("hi", "xlo"), axis=0, tiled=True)
+    normed_half = lax.all_gather(normed_row, "z", axis=0, tiled=True)
     hidden_units = gate_both.shape[1]
     part_gate = jnp.dot(normed_half, gate_both, preferred_element_type=jnp.float32)
     part_upward = jnp.dot(normed_half, up_both, preferred_element_type=jnp.float32)
@@ -171,9 +173,8 @@
     act = (jax.nn.silu(gate) * upward).astype(jnp.bfloat16)
     act_all = lax.all_gather(act, "grp", axis=0, tiled=True)
     down = jnp.dot(act_all, down_both, preferred_element_type=jnp.float32)
-    returned = lax.psum_scatter(
-        down.astype(jnp.bfloat16), ("hi", "tp"), scatter_dimension=0, tiled=True
-    )
+    returned = lax.psum_scatter(down.astype(jnp.bfloat16), "z", scatter_dimension=0, tiled=True)
+    returned = lax.psum_scatter(returned, ("hi", "xlo"), scatter_dimension=0, tiled=True)
     return (middle_float + returned.astype(jnp.float32)).astype(jnp.bfloat16)
 
 
@@ -181,9 +182,9 @@
     pool = ("hi", "core")
     chip_mesh = jax.sharding.Mesh(
         mesh.devices.reshape(
-            mesh.shape["pool"] // 2, 2, mesh.shape["grp"], mesh.shape["tp"]
+            mesh.shape["pool"] // 2, 2, mesh.shape["grp"], mesh.shape["tp"] // 2, 2
         ),
-        ("hi", "core", "grp", "tp"),
+        ("hi", "core", "grp", "z", "xlo"),
     )
     return jax.shard_map(
         body,
@@ -191,21 +192,21 @@
         in_specs=(
             P(pool, "grp"),
             P("grp"),
-            P("grp", "tp"),
-            P("grp", "tp"),
-            P("grp", "tp"),
-            P("tp", "grp"),
-            P(pool, "grp", "tp"),
-            P(pool, "grp", "tp"),
-            P(pool, "grp", "tp"),
-            P(pool, "grp", "tp"),
+            P("grp", TP),
+            P("grp", TP),
+            P("grp", TP),
+            P(TP, "grp"),
+            P(pool, "grp", TP),
+            P(pool, "grp", TP),
+            P(pool, "grp", TP),
+            P(pool, "grp", TP),
             P(pool),
             P(pool),
             P("grp"),
-            P("grp", pool + ("tp",)),
-            P("grp", pool + ("tp",)),
-            P(pool + ("tp",), "grp"),
+            P("grp", pool + TP),
+            P("grp", pool + TP),
+            P(pool + TP, "grp"),
         ),
-        out_specs=P(pool + ("tp",), "grp"),
+        out_specs=P(pool + TP, "grp"),
         check_vma=False,
     )

time: 453 us -> 391 us (0.86)
  waiting for transfers between devices: 245 us -> 170 us
  blocking collectives: 96.7 us -> 110 us
    all_gather x1, waiting for transfers between devices: 67.8 us -> 21.4 us  [body(): normed_half = lax.all_gather(normed_row, 'z', axis=0, tiled=True)]
    reduce_scatter x2 -> x3, waiting for transfers between devices: 121 us -> 93.2 us  [the longest x1 40.1 us: body(): lax.psum_scatter(partial_out.astype(jnp.bfloat16), TP, scatter_dimension=...]
    all_gather x0 -> x1, blocking collectives: none -> 13.5 us  [body(): normed_row = lax.all_gather(normed_own, ('hi', 'xlo'), axis=0, tiled=True)]
  transfers between devices with their start and end apart: 8 -> 9, of which waited for: 6 -> 7; matrix products, arithmetic and copies ran while one was open for 2% -> 2% of each run, Pallas kernels for 0% -> 0%
where the time goes in v4:
time: 391 us
  waiting for transfers between devices  170 us (43%)
  blocking collectives  110 us (28%)
  matrix products  61.6 us (16%)
  local copies, waits for them, and re-layouts  18.2 us (5%)
  other arithmetic  15.6 us (4%)
  between operations  13.8 us (4%)
    reduce_scatter x1, waiting for transfers between devices, body(): lax.psum_scatter(partial_out.astype(jnp.bfloat16), TP, scatter_dimension=...  40.1 us
    psum x1, blocking collectives, body(): lax.psum((part_query, part_key, part_value), 'grp')  30.7 us
    reduce_scatter x1, waiting for transfers between devices, body(): lax.psum_scatter(down.astype(jnp.bfloat16), 'z', scatter_dimension=0, til...  29.7 us
    reduce_scatter x1, waiting for transfers between devices, body(): lax.psum_scatter(both, 'grp', scatter_dimension=0, tiled=True)  27.4 us
    reduce_scatter x1, waiting for transfers between devices, body(): reduced = lax.psum_scatter(packed, 'grp', scatter_dimension=0, tiled=True)  24.8 us
    reduce_scatter x1, waiting for transfers between devices, body(): lax.psum_scatter(returned, ('hi', 'xlo'), scatter_dimension=0, tiled=True)  23.4 us
    all_gather x1, waiting for transfers between devices, body(): normed_half = lax.all_gather(normed_row, 'z', axis=0, tiled=True)  21.4 us
    pmax x1, blocking collectives, body(): lax.pmax(jnp.maximum(jnp.maximum(pre_peak, suf_scores.max(axis=3)), own_s...  17.3 us
  transfers between devices with their start and end apart: 9, of which 7 were waited for; matrix products, arithmetic and copies ran while one was open for 2% of the time, Pallas kernels for 0%

profile of v4, /device:TPU:0, one launch (start us, length us, event | category | flops | bytes accessed | tf_op | source)
XLA Modules:
  0.0 390.7 jit_solution(743277726016506701)
XLA Ops:
  12.8 10.9 %psum.35 = f32[256]{0:T(256)S(1)} all-reduce(f32[256]{0:T(256)S(1)} %multiply_reduce_fusion), channel_id=1, replica_groups=mesh['hi'=2,'core'=2,'grp'=4,'z'=4,'xlo'=2] {'grp'}, use_global_device_ids=true, to_apply=%region_1.0 | all-reduce | flops 256 | bytes 2048 | tf_op jit(solution)/shard_map/psum | solution.py:57
  23.7 3.9 %fusion.60 = f32[256,1024]{1,0:T(8,128)S(1)} fusion(bf16[2048,1024]{1,0:T(8,128)(2,1)} %param.20, f32[2048]{0:T(1024)} %param.19, f32[256]{0:T(256)S(1)} %add_rsqrt_fusion, bf16[256,2048]{1,0:T(8,128)(2,1)} %param.18), kind=kOutput, calls=%fused_computation.101 | convolution fusion | flops 1075838976 | bytes 6300672 | tf_op jit(solution)/shard_map/dot_general | solution.py:60
  29.2 30.7 %all-reduce.2 = (bf16[256,1024]{1,0:T(8,128)(2,1)}, bf16[256,128]{1,0:T(8,128)(2,1)S(1)}, bf16[256,128]{1,0:T(8,128)(2,1)S(1)}) all-reduce(f32[256,1024]{1,0:T(8,128)S(1)} %fusion.60, f32[256,128]{1,0:T(8,128)S(1)} %fusion.59, f32[256,128]{1,0:T(8,128)S(1)} %fusion.58), channel_id=1, replica_groups=mesh['hi'=2,'core'=2,'grp'=4,'z'=4,'xlo'=2] {'grp'}, use_global_device_ids=true, to_apply=%region_2.0 | all-reduce | flops 327680 | bytes 1966080 | tf_op jit(solution)/shard_map/psum | solution.py:63
  61.9 13.1 %bitcast_reduce_fusion = (f32[2,128,8]{1,2,0:T(8,128)S(1)}, f32[2,128,8,4096]{3,1,2,0:T(8,128)}) fusion(bf16[2,4096,128]{2,1,0:T(8,128)(2,1)S(1)} %copy-done, bf16[2,128,8,128]{3,2,1,0:T(8,128)(2,1)S(1)} %bitcast.133), kind=kOutput, calls=%fused_computation.6 | convolution fusion | flops 2164258816 | bytes 36184064 | tf_op jit(solution)/shard_map/pskgd,pjkd->pskgj/dot_general | solution.py:94
  76.4 4.5 %fusion.62 = (f32[256,8]{1,0:T(8,128)S(1)}, f32[256,8,64]{2,1,0:T(8,128)S(1)}) fusion(bf16[256,8,128]{2,1,0:T(8,128)(2,1)S(1)} %bitcast.130, bf16[256,64,128]{2,1,0:T(8,128)(2,1)} %param.26, pred[256,64]{1,0:T(8,128)(4,1)S(1)} %broadcast_compare_fusion), kind=kOutput, calls=%fused_computation.102 | convolution fusion | flops 33945600 | bytes 5267456 | tf_op jit(solution)/shard_map/skgd,sjkd->skgj/dot_general | solution.py:101
  81.0 17.3 %pmax.7 = f32[256,1,8]{2,0,1:T(8,128)S(1)} all-reduce(f32[256,1,8]{2,0,1:T(8,128)S(1)} %get-tuple-element.25), channel_id=1, replica_groups=mesh['hi'=2,'core'=2,'grp'=4,'z'=4,'xlo'=2] {'grp'}, use_global_device_ids=true, to_apply=%region_10.11 | all-reduce | flops 2048 | bytes 16384 | tf_op jit(solution)/shard_map/pmax | solution.py:113
  99.1 15.1 %fusion.26 = f32[2,128,1,8,256]{4,1,3,0,2:T(8,128)} fusion(f32[2,128,8,4096]{3,1,2,0:T(8,128)} %get-tuple-element.27, f32[2,128,8]{1,2,0:T(8,128)S(1)} %copy.26, bf16[2,4096,1,128]{3,1,0,2:T(8,128)(2,1)} %bitcast.140, bf16[256]{0:T(256)(128)(2,1)S(1)} %pad.13.clone), kind=kOutput, calls=%fused_computation.35 | convolution fusion | flops 4328521728 | bytes 37757440 | tf_op jit(solution)/shard_map/pskgj,pjkd->pskgd/dot_general | solution.py:120
  114.2 4.2 %copy.27 = f32[2,128,1,8,256]{4,3,1,0,2:T(8,128)} copy(f32[2,128,1,8,256]{4,1,3,0,2:T(8,128)} %fusion.26) | data formatting | bytes 4194304 | tf_op jit(solution)/shard_map/pskgj,pjkd->pskgd/transpose | solution.py:120
  118.4 3.6 gather_fusion.3
  130.8 24.8 %reduce-scatter.6.cloned.1.call-done = f32[64,1032]{1,0:T(8,128)} async-done(((f32[256,1032]{1,0:T(8,128)}), f32[64,1032]{1,0:T(8,128)}) %reduce-scatter.6.cloned.1.call-update) | async-done | bytes 264208 | tf_op jit(solution)/shard_map/reduce_scatter | solution.py:133
  157.6 12.8 %all_gather.12 = bf16[256,1024]{1,0:T(8,128)(2,1)S(1)} all-gather(bf16[64,1024]{1,0:T(8,128)(2,1)S(1)} %fusion.43), channel_id=1, replica_groups=mesh['hi'=2,'core'=2,'grp'=4,'z'=4,'xlo'=2] {'grp'}, dimensions={0}, use_global_device_ids=true | all-gather | bytes 655360 | tf_op jit(solution)/shard_map/all_gather | solution.py:147
  170.4 4.5 %convolution_convert_fusion = bf16[256,2048]{1,0:T(8,128)(2,1)} fusion(bf16[256,1024]{1,0:T(8,128)(2,1)S(1)} %all_gather.12, bf16[1024,2048]{1,0:T(8,128)(2,1)} %param.23), kind=kOutput, calls=%fused_computation.28 | convolution fusion | flops 1074266112 | bytes 5767168 | tf_op jit(solution)/shard_map/dot_general | solution.py:148
  176.6 40.1 %reduce-scatter.8.cloned.1.call-done = bf16[32,2048]{1,0:T(8,128)(2,1)} async-done(((bf16[256,2048]{1,0:T(8,128)(2,1)}), bf16[32,2048]{1,0:T(8,128)(2,1)}) %reduce-scatter.8.cloned.1.call-update) | async-done | bytes 131088 | tf_op jit(solution)/shard_map/reduce_scatter | solution.py:151
  217.8 10.5 %psum.39 = f32[32]{0:T(128)S(1)} all-reduce(f32[32]{0:T(128)S(1)} %get-tuple-element.20), channel_id=1, replica_groups=mesh['hi'=2,'core'=2,'grp'=4,'z'=4,'xlo'=2] {'grp'}, use_global_device_ids=true, to_apply=%region_16.17 | all-reduce | flops 32 | bytes 256 | tf_op jit(solution)/shard_map/psum | solution.py:157
  228.4 13.5 %all_gather.13 = bf16[128,2048]{1,0:T(8,128)(2,1)} all-gather(bf16[32,2048]{1,0:T(8,128)(2,1)S(1)} %fusion.41), channel_id=1, replica_groups=mesh['hi'=2,'core'=2,'grp'=4,'z'=4,'xlo'=2] {'hi','xlo'}, dimensions={0}, use_global_device_ids=true | all-gather | bytes 655360 | tf_op jit(solution)/shard_map/all_gather | solution.py:164
  242.6 3.5 collective-permute-done.1
  247.3 21.4 %all-gather.2.cloned.1.call-done = bf16[512,2048]{1,0:T(8,128)(2,1)} async-done(((bf16[128,2048]{1,0:T(8,128)(2,1)}), bf16[512,2048]{1,0:T(8,128)(2,1)}) %all-gather.2.cloned.1.call-update) | async-done | bytes 2097168 | tf_op jit(solution)/shard_map/all_gather | solution.py:165
  268.7 5.2 %fusion.29 = bf16[512,896]{1,0:T(8,128)(2,1)S(1)} fusion(bf16[512,2048]{1,0:T(8,128)(2,1)} %all-gather.2.cloned.1.call-done, bf16[2048,448]{0,1:T(8,128)(2,1)} %copy-done.8, bf16[2048,448]{0,1:T(8,128)(2,1)} %param.32), kind=kOutput, calls=%fused_computation.36 | convolution fusion | flops 1886846976 | bytes 6684672 | tf_op jit(solution)/shard_map/dot_general | solution.py:168
  273.9 4.4 %fusion.32 = bf16[512,896]{1,0:T(8,128)(2,1)S(1)} fusion(bf16[512,2048]{1,0:T(8,128)(2,1)S(1)} %copy-done.7, bf16[2048,448]{0,1:T(8,128)(2,1)} %collective-permute-done, bf16[2048,448]{0,1:T(8,128)(2,1)} %param.31), kind=kOutput, calls=%fused_computation.37 | convolution fusion | flops 1886846976 | bytes 6684672 | tf_op jit(solution)/shard_map/dot_general | solution.py:167
  279.9 27.4 %reduce-scatter.10.cloned.1.call-done = bf16[128,1792]{1,0:T(8,128)(2,1)} async-done(((bf16[512,1792]{1,0:T(8,128)(2,1)}), bf16[128,1792]{1,0:T(8,128)(2,1)}) %reduce-scatter.10.cloned.1.call-update) | async-done | bytes 458768 | tf_op jit(solution)/shard_map/reduce_scatter | solution.py:170
  308.6 14.6 %all_gather.15 = bf16[512,896]{1,0:T(8,128)(2,1)S(1)} all-gather(bf16[128,896]{1,0:T(8,128)(2,1)S(1)} %fusion.38), channel_id=1, replica_groups=mesh['hi'=2,'core'=2,'grp'=4,'z'=4,'xlo'=2] {'grp'}, dimensions={0}, use_global_device_ids=true | all-gather | bytes 1146880 | tf_op jit(solution)/shard_map/all_gather | solution.py:174
  323.1 5.9 %fusion.20 = bf16[512,2048]{1,0:T(8,128)(2,1)} fusion(bf16[512,896]{1,0:T(8,128)(2,1)S(1)} %all_gather.15, bf16[448,2048]{1,0:T(8,128)(2,1)} %collective-permute-done.2, bf16[448,2048]{1,0:T(8,128)(2,1)} %param.33), kind=kOutput, calls=%fused_computation.27 | convolution fusion | flops 1887436800 | bytes 6684672 | tf_op jit(solution)/shard_map/dot_general | solution.py:175
  329.1 29.7 %reduce-scatter.12.cloned.1.call-done = bf16[128,2048]{1,0:T(8,128)(2,1)} async-done(((bf16[512,2048]{1,0:T(8,128)(2,1)}), bf16[128,2048]{1,0:T(8,128)(2,1)}) %reduce-scatter.12.cloned.1.call-update) | async-done | bytes 524304 | tf_op jit(solution)/shard_map/reduce_scatter | solution.py:176
  358.9 23.4 %reduce-scatter.14.cloned.1.call-done = bf16[32,2048]{1,0:T(8,128)(2,1)} async-done(((bf16[128,2048]{1,0:T(8,128)(2,1)}), bf16[32,2048]{1,0:T(8,128)(2,1)}) %reduce-scatter.14.cloned.1.call-update) | async-done | bytes 131088 | tf_op jit(solution)/shard_map/reduce_scatter | solution.py:177
  (93 shorter events, 31.9 us)
Async XLA Ops:
  6.5 55.3 %copy-start = (bf16[2,4096,128]{2,1,0:T(8,128)(2,1)S(1)}, bf16[2,4096,128]{2,1,0:T(8,128)(2,1)}, u32[]{:S(2)}) copy-start(bf16[2,4096,128]{2,1,0:T(8,128)(2,1)} %param.24) | copy-start | bytes 6291460
  6.5 149.1 %reduce-scatter.6.cloned.1.call-start = ((), (), s32[]{:S(2)}) async-start(), calls=%async_computation.5 | async-start | bytes 1474560 | tf_op jit(solution)/shard_map/reduce_scatter | solution.py:133
  23.7 4.0 %copy-start.3 = (bf16[256,2048]{1,0:T(8,128)(2,1)S(1)}, bf16[256,2048]{1,0:T(8,128)(2,1)}, u32[]{:S(2)}) copy-start(bf16[256,2048]{1,0:T(8,128)(2,1)} %param.18) | copy-start | bytes 3145732
  23.7 4.0 %copy-start.9 = (bf16[2048,128]{1,0:T(8,128)(2,1)S(1)}, bf16[2048,128]{1,0:T(8,128)(2,1)}, u32[]{:S(2)}) copy-start(bf16[2048,128]{1,0:T(8,128)(2,1)} %param.22) | copy-start | bytes 1572868
  23.7 4.0 %copy-start.11 = (f32[2048]{0:T(1024)S(1)}, f32[2048]{0:T(1024)}, u32[]{:S(2)}) copy-start(f32[2048]{0:T(1024)} %param.19) | copy-start | bytes 24580
  27.7 1.0 copy-start.10
  75.0 1.3 copy-start.6
  80.9 18.1 %copy-start.12 = (bf16[128]{0:T(256)(128)(2,1)S(1)}, bf16[128]{0:T(256)(128)(2,1)}, u32[]{:S(2)}) copy-start(bf16[128]{0:T(256)(128)(2,1)} %constant.77.clone.1) | copy-start | bytes 772
  122.0 2.2 copy-start.2
  130.6 86.1 %reduce-scatter.8.cloned.1.call-start = ((), (), s32[]{:S(2)}) async-start(), calls=%async_computation.6 | async-start | bytes 1179648 | tf_op jit(solution)/shard_map/reduce_scatter | solution.py:151
  170.4 4.6 %copy-start.4 = (bf16[256,2048]{1,0:T(8,128)(2,1)S(1)}, bf16[256,2048]{1,0:T(8,128)(2,1)}, u32[]{:S(2)}) copy-start(bf16[256,2048]{1,0:T(8,128)(2,1)} %param.18) | copy-start | bytes 3145732
  174.9 53.4 %copy-start.5 = (f32[2048]{0:T(1024)S(1)}, f32[2048]{0:T(1024)}, u32[]{:S(2)}) copy-start(f32[2048]{0:T(1024)} %param.30) | copy-start | bytes 24580
  174.9 93.8 %all-gather.2.cloned.1.call-start = ((), (), s32[]{:S(2)}) async-start(), calls=%async_computation.7 | async-start | bytes 2621440 | tf_op jit(solution)/shard_map/all_gather | solution.py:165
  242.0 65.4 %reduce-scatter.10.cloned.1.call-start = ((), (), s32[]{:S(2)}) async-start(), calls=%async_computation.8 | async-start | bytes 2293760 | tf_op jit(solution)/shard_map/reduce_scatter | solution.py:170
  242.0 4.1 %collective-permute-start.1 = (bf16[2048,448]{0,1:T(8,128)(2,1)}, bf16[2048,448]{0,1:T(8,128)(2,1)S(1)}, u32[]{:S(2)}, u32[]{:S(2)}) collective-permute-start(bf16[2048,448]{0,1:T(8,128)(2,1)} %param.32), channel_id=1, source_target_pairs={{0,32},{32,0},{1,33},{33,1},{2,34},{34,2},{3,35},{35,3},{4,36},{36... | collective-permute-start | bytes 5505032 | tf_op jit(solution)/shard_map/ppermute | solution.py:162
  242.1 31.8 %collective-permute-start = (bf16[2048,448]{0,1:T(8,128)(2,1)}, bf16[2048,448]{0,1:T(8,128)(2,1)}, u32[]{:S(2)}, u32[]{:S(2)}) collective-permute-start(bf16[2048,448]{0,1:T(8,128)(2,1)} %param.31), channel_id=1, source_target_pairs={{0,32},{32,0},{1,33},{33,1},{2,34},{34,2},{3,35},{35,3},{4,36},{36... | collective-permute-start | bytes 5505032 | tf_op jit(solution)/shard_map/ppermute | solution.py:161
  246.1 1.3 copy-start.8
  268.7 5.2 %copy-start.7 = (bf16[512,2048]{1,0:T(8,128)(2,1)S(1)}, bf16[512,2048]{1,0:T(8,128)(2,1)}, u32[]{:S(2)}) copy-start(bf16[512,2048]{1,0:T(8,128)(2,1)} %all-gather.2.cloned.1.call-done) | copy-start | bytes 6291460
  279.8 79.1 %reduce-scatter.12.cloned.1.call-start = ((), (), s32[]{:S(2)}) async-start(), calls=%async_computation.9 | async-start | bytes 2621440 | tf_op jit(solution)/shard_map/reduce_scatter | solution.py:176
  279.8 43.3 %collective-permute-start.2 = (bf16[448,2048]{1,0:T(8,128)(2,1)}, bf16[448,2048]{1,0:T(8,128)(2,1)}, u32[]{:S(2)}, u32[]{:S(2)}) collective-permute-start(bf16[448,2048]{1,0:T(8,128)(2,1)} %param.33), channel_id=1, source_target_pairs={{0,32},{32,0},{1,33},{33,1},{2,34},{34,2},{3,35},{35,3},{4,36},{36... | collective-permute-start | bytes 5505032 | tf_op jit(solution)/shard_map/ppermute | solution.py:163
  323.1 60.8 %copy-start.1 = (bf16[2,4096,128]{2,1,0:T(8,128)(2,1)S(1)}, bf16[2,4096,128]{2,1,0:T(8,128)(2,1)}, u32[]{:S(2)}) copy-start(bf16[2,4096,128]{2,1,0:T(8,128)(2,1)} %param.24) | copy-start | bytes 6291460
  329.1 53.2 %reduce-scatter.14.cloned.1.call-start = ((), (), s32[]{:S(2)}) async-start(), calls=%async_computation.10 | async-start | bytes 655360 | tf_op jit(solution)/shard_map/reduce_scatter | solution.py:177
Sparse Core Ops, SparseCore 0:
  130.7 24.8 reduce-scatter.5
  175.0 41.5 reduce-scatter.7
  242.1 26.5 all-gather.1
  279.9 27.4 reduce-scatter.9
  329.2 29.6 reduce-scatter.11
  361.1 21.1 reduce-scatter.13

commit v5 on v4

--- a/solution.py
+++ b/solution.py
@@ -130,21 +130,15 @@
     )
     flat = stream_count, kv_local * groups
     packed = jnp.concatenate([numer.reshape(stream_count, -1), total.reshape(flat)], axis=1)
-    reduced = lax.psum_scatter(packed, "grp", scatter_dimension=0, tiled=True)
-    quarter = reduced.shape[0]
-    q_start = lax.axis_index("grp") * quarter
+    reduced = lax.psum(packed, "grp")
     width = kv_local * groups * HD
-    numer = reduced[:, :width].reshape(quarter, kv_local, groups, HD)
-    total = reduced[:, width:].reshape(quarter, kv_local, groups)
-    own_score = lax.dynamic_slice_in_dim(own_score, q_start, quarter, 0)
-    own_peak = lax.dynamic_slice_in_dim(peak, q_start, quarter, 0)
-    own_weight = jnp.exp(own_score - own_peak).astype(jnp.bfloat16).astype(jnp.float32)
+    numer = reduced[:, :width].reshape(stream_count, kv_local, groups, HD)
+    total = reduced[:, width:].reshape(stream_count, kv_local, groups)
+    own_weight = jnp.exp(own_score - peak).astype(jnp.bfloat16).astype(jnp.float32)
     total = total + own_weight
-    own_value = lax.dynamic_slice_in_dim(value_new, q_start, quarter, 0)
-    own_value = own_value.reshape(quarter, kv_local, 1, HD).astype(jnp.float32)
+    own_value = value_new.reshape(stream_count, kv_local, 1, HD).astype(jnp.float32)
     numer = numer + own_weight[..., None] * own_value
-    attended = (numer / total[..., None]).reshape(quarter, q_local * HD).astype(jnp.bfloat16)
-    attended = lax.all_gather(attended, "grp", axis=0, tiled=True)
+    attended = (numer / total[..., None]).reshape(stream_count, q_local * HD).astype(jnp.bfloat16)
     partial_out = jnp.dot(attended, w_out, preferred_element_type=jnp.float32)
     share = stream_count // (lax.axis_size("z") * lax.axis_size("xlo"))
     tp_start = (lax.axis_index("z") * lax.axis_size("xlo") + lax.axis_index("xlo")) * share
@@ -167,12 +161,11 @@
     part_gate = jnp.dot(normed_half, gate_both, preferred_element_type=jnp.float32)
     part_upward = jnp.dot(normed_half, up_both, preferred_element_type=jnp.float32)
     both = jnp.concatenate([part_gate, part_upward], axis=1).astype(jnp.bfloat16)
-    reduced = lax.psum_scatter(both, "grp", scatter_dimension=0, tiled=True).astype(jnp.float32)
+    reduced = lax.psum(both, "grp").astype(jnp.float32)
     gate = reduced[:, :hidden_units]
     upward = reduced[:, hidden_units:]
     act = (jax.nn.silu(gate) * upward).astype(jnp.bfloat16)
-    act_all = lax.all_gather(act, "grp", axis=0, tiled=True)
-    down = jnp.dot(act_all, down_both, preferred_element_type=jnp.float32)
+    down = jnp.dot(act, down_both, preferred_element_type=jnp.float32)
     returned = lax.psum_scatter(down.astype(jnp.bfloat16), "z", scatter_dimension=0, tiled=True)
     returned = lax.psum_scatter(returned, ("hi", "xlo"), scatter_dimension=0, tiled=True)
     return (middle_float + returned.astype(jnp.float32)).astype(jnp.bfloat16)

time: 391 us -> 415 us (1.061)
  waiting for transfers between devices: 170 us -> 221 us
  blocking collectives: 110 us -> 82.9 us
    psum x0 -> x2, waiting for transfers between devices: none -> 101 us  [the longest x1 54.3 us: body(): reduced = lax.psum(both, 'grp').astype(jnp.float32)]
    reduce_scatter x2 -> x0, waiting for transfers between devices: 52.2 us -> none  [the longest x1 27.4 us: body(): lax.psum_scatter(both, 'grp', scatter_dimension=0, tiled=True)]
    all_gather x2 -> x0, blocking collectives: 27.4 us -> none  [the longest x1 14.6 us: body(): act_all = lax.all_gather(act, 'grp', axis=0, tiled=True)]
where the time goes in v5:
time: 415 us; the launch traced here: 414 us
  waiting for transfers between devices  221 us (53%)
  blocking collectives  82.9 us (20%)
  matrix products  62.1 us (15%)
  local copies, waits for them, and re-layouts  18.4 us (4%)
  other arithmetic  15.5 us (4%)
  between operations  13.8 us (3%)
    psum x1, waiting for transfers between devices, body(): reduced = lax.psum(both, 'grp').astype(jnp.float32)  54.3 us
    psum x1, waiting for transfers between devices, body(): reduced = lax.psum(packed, 'grp')  46.9 us
    reduce_scatter x1, waiting for transfers between devices, body(): lax.psum_scatter(partial_out.astype(jnp.bfloat16), TP, scatter_dimension=...  41.2 us
    psum x1, blocking collectives, body(): lax.psum((part_query, part_key, part_value), 'grp')  30.7 us
    reduce_scatter x1, waiting for transfers between devices, body(): lax.psum_scatter(down.astype(jnp.bfloat16), 'z', scatter_dimension=0, til...  29.8 us
    reduce_scatter x1, waiting for transfers between devices, body(): lax.psum_scatter(returned, ('hi', 'xlo'), scatter_dimension=0, tiled=True)  23.5 us
    all_gather x1, waiting for transfers between devices, body(): normed_half = lax.all_gather(normed_row, 'z', axis=0, tiled=True)  21.4 us
    pmax x1, blocking collectives, body(): lax.pmax(jnp.maximum(jnp.maximum(pre_peak, suf_scores.max(axis=3)), own_s...  17.3 us
  transfers between devices with their start and end apart: 9, of which 7 were waited for; matrix products, arithmetic and copies ran while one was open for 2% of the time, Pallas kernels for 0%

profile of v5, /device:TPU:0, one launch (start us, length us, event | category | flops | bytes accessed | tf_op | source)
XLA Modules:
  0.0 414.3 jit_solution(11966698531848108941)
XLA Ops:
  12.8 10.9 %psum.49 = f32[256]{0:T(256)S(1)} all-reduce(f32[256]{0:T(256)S(1)} %multiply_reduce_fusion), channel_id=1, replica_groups=mesh['hi'=2,'core'=2,'grp'=4,'z'=4,'xlo'=2] {'grp'}, use_global_device_ids=true, to_apply=%region_1.0 | all-reduce | flops 256 | bytes 2048 | tf_op jit(solution)/shard_map/psum | solution.py:57
  23.7 3.9 fusion.63
  29.2 30.7 %all-reduce.8 = (bf16[256,1024]{1,0:T(8,128)(2,1)}, bf16[256,128]{1,0:T(8,128)(2,1)S(1)}, bf16[256,128]{1,0:T(8,128)(2,1)S(1)}) all-reduce(f32[256,1024]{1,0:T(8,128)S(1)} %fusion.63, f32[256,128]{1,0:T(8,128)S(1)} %fusion.62, f32[256,128]{1,0:T(8,128)S(1)} %fusion.61), channel_id=1, replica_groups=mesh['hi'=2,'core'=2,'grp'=4,'z'=4,'xlo'=2] {'grp'}, use_global_device_ids=true, to_apply=%region_2.0 | all-reduce | flops 327680 | bytes 1966080 | tf_op jit(solution)/shard_map/psum | solution.py:63
  61.9 13.1 %bitcast_reduce_fusion = (f32[2,128,8]{1,2,0:T(8,128)S(1)}, f32[2,128,8,4096]{3,1,2,0:T(8,128)}) fusion(bf16[2,4096,128]{2,1,0:T(8,128)(2,1)S(1)} %copy-done, bf16[2,128,8,128]{3,2,1,0:T(8,128)(2,1)S(1)} %bitcast.133), kind=kOutput, calls=%fused_computation.6 | convolution fusion | flops 2164258816 | bytes 36184064 | tf_op jit(solution)/shard_map/pskgd,pjkd->pskgj/dot_general | solution.py:94
  76.4 4.5 %fusion.65 = (f32[256,8]{1,0:T(8,128)S(1)}, f32[256,8,64]{2,1,0:T(8,128)S(1)}) fusion(bf16[256,8,128]{2,1,0:T(8,128)(2,1)S(1)} %bitcast.130, bf16[256,64,128]{2,1,0:T(8,128)(2,1)} %param.26, pred[256,64]{1,0:T(8,128)(4,1)S(1)} %broadcast_compare_fusion), kind=kOutput, calls=%fused_computation.102 | convolution fusion | flops 33945600 | bytes 5267456 | tf_op jit(solution)/shard_map/skgd,sjkd->skgj/dot_general | solution.py:101
  81.0 17.3 %pmax.7 = f32[256,1,8]{2,0,1:T(8,128)S(1)} all-reduce(f32[256,1,8]{2,0,1:T(8,128)S(1)} %maximum_bitcast_fusion.4), channel_id=1, replica_groups=mesh['hi'=2,'core'=2,'grp'=4,'z'=4,'xlo'=2] {'grp'}, use_global_device_ids=true, to_apply=%region_10.11 | all-reduce | flops 2048 | bytes 16384 | tf_op jit(solution)/shard_map/pmax | solution.py:113
  99.1 15.1 %fusion.27 = f32[2,128,1,8,256]{4,1,3,0,2:T(8,128)} fusion(f32[2,128,8,4096]{3,1,2,0:T(8,128)} %get-tuple-element.25, f32[2,128,8]{1,2,0:T(8,128)S(1)} %copy.26, bf16[2,4096,1,128]{3,1,0,2:T(8,128)(2,1)} %bitcast.141, bf16[256]{0:T(256)(128)(2,1)S(1)} %pad.13.clone), kind=kOutput, calls=%fused_computation.37 | convolution fusion | flops 4328521728 | bytes 37757440 | tf_op jit(solution)/shard_map/pskgj,pjkd->pskgd/dot_general | solution.py:120
  114.2 4.2 %copy.27 = f32[2,128,1,8,256]{4,3,1,0,2:T(8,128)} copy(f32[2,128,1,8,256]{4,1,3,0,2:T(8,128)} %fusion.27) | data formatting | bytes 4194304 | tf_op jit(solution)/shard_map/pskgj,pjkd->pskgd/transpose | solution.py:120
  118.4 3.6 gather_fusion.3
  124.2 3.5 fusion.36
  131.1 46.9 %all-reduce.5.cloned.1.call-done = f32[256,1032]{1,0:T(8,128)} async-done(((f32[256,1032]{1,0:T(8,128)}), f32[256,1032]{1,0:T(8,128)}) %all-reduce.5.cloned.1.call-update) | async-done | bytes 1056784 | tf_op jit(solution)/shard_map/psum | solution.py:133
  179.3 5.0 %convolution_convert_fusion = bf16[256,2048]{1,0:T(8,128)(2,1)} fusion(bf16[1024,2048]{1,0:T(8,128)(2,1)} %param.23, f32[32,8,8,128]{3,2,1,0:T(8,128)S(1)} %bitcast.135, f32[32,8,8,128]{3,2,1,0:T(8,128)S(1)} %bitcast.134, f32[256,1032]{1,0:T(8,128)} %all-reduce.5.cloned.1.call-done), kind=kOutput, calls=%fused_computation.28 | convolution fusion | flops 1075052544 | bytes 8388608 | tf_op jit(solution)/shard_map/dot_general | solution.py:142
  185.9 41.2 %reduce-scatter.4.cloned.1.call-done = bf16[32,2048]{1,0:T(8,128)(2,1)} async-done(((bf16[256,2048]{1,0:T(8,128)(2,1)}), bf16[32,2048]{1,0:T(8,128)(2,1)}) %reduce-scatter.4.cloned.1.call-update) | async-done | bytes 131088 | tf_op jit(solution)/shard_map/reduce_scatter | solution.py:145
  228.3 10.5 %psum.54 = f32[32]{0:T(128)S(1)} all-reduce(f32[32]{0:T(128)S(1)} %get-tuple-element.20), channel_id=1, replica_groups=mesh['hi'=2,'core'=2,'grp'=4,'z'=4,'xlo'=2] {'grp'}, use_global_device_ids=true, to_apply=%region_16.17 | all-reduce | flops 32 | bytes 256 | tf_op jit(solution)/shard_map/psum | solution.py:151
  239.0 13.5 %all_gather.6 = bf16[128,2048]{1,0:T(8,128)(2,1)} all-gather(bf16[32,2048]{1,0:T(8,128)(2,1)S(1)} %fusion.45), channel_id=1, replica_groups=mesh['hi'=2,'core'=2,'grp'=4,'z'=4,'xlo'=2] {'hi','xlo'}, dimensions={0}, use_global_device_ids=true | all-gather | bytes 655360 | tf_op jit(solution)/shard_map/all_gather | solution.py:158
  253.2 3.5 collective-permute-done.1
  257.9 21.4 %all-gather.2.cloned.1.call-done = bf16[512,2048]{1,0:T(8,128)(2,1)} async-done(((bf16[128,2048]{1,0:T(8,128)(2,1)}), bf16[512,2048]{1,0:T(8,128)(2,1)}) %all-gather.2.cloned.1.call-update) | async-done | bytes 2097168 | tf_op jit(solution)/shard_map/all_gather | solution.py:159
  279.3 5.2 %fusion.30 = bf16[512,896]{1,0:T(8,128)(2,1)S(1)} fusion(bf16[512,2048]{1,0:T(8,128)(2,1)} %all-gather.2.cloned.1.call-done, bf16[2048,448]{0,1:T(8,128)(2,1)} %copy-done.8, bf16[2048,448]{0,1:T(8,128)(2,1)} %param.32), kind=kOutput, calls=%fused_computation.38 | convolution fusion | flops 1886846976 | bytes 6684672 | tf_op jit(solution)/shard_map/dot_general | solution.py:162
  284.6 4.4 %fusion.33 = bf16[512,896]{1,0:T(8,128)(2,1)S(1)} fusion(bf16[512,2048]{1,0:T(8,128)(2,1)S(1)} %copy-done.7, bf16[2048,448]{0,1:T(8,128)(2,1)} %collective-permute-done, bf16[2048,448]{0,1:T(8,128)(2,1)} %param.31), kind=kOutput, calls=%fused_computation.39 | convolution fusion | flops 1886846976 | bytes 6684672 | tf_op jit(solution)/shard_map/dot_general | solution.py:161
  290.5 54.3 %all-reduce.7.cloned.1.call-done = bf16[512,1792]{1,0:T(8,128)(2,1)} async-done(((bf16[512,1792]{1,0:T(8,128)(2,1)}), bf16[512,1792]{1,0:T(8,128)(2,1)}) %all-reduce.7.cloned.1.call-update) | async-done | bytes 1835024 | tf_op jit(solution)/shard_map/psum | solution.py:164
  344.8 1.8 convert_element_type.93
  346.6 5.9 %fusion.20 = bf16[512,2048]{1,0:T(8,128)(2,1)} fusion(bf16[448,2048]{1,0:T(8,128)(2,1)} %collective-permute-done.2, bf16[448,2048]{1,0:T(8,128)(2,1)} %param.33, f32[512,1792]{1,0:T(8,128)S(1)} %convert_element_type.93), kind=kOutput, calls=%fused_computation.27 | convolution fusion | flops 1890189312 | bytes 9437184 | tf_op jit(solution)/shard_map/dot_general | solution.py:168
  352.6 29.8 %reduce-scatter.6.cloned.1.call-done = bf16[128,2048]{1,0:T(8,128)(2,1)} async-done(((bf16[512,2048]{1,0:T(8,128)(2,1)}), bf16[128,2048]{1,0:T(8,128)(2,1)}) %reduce-scatter.6.cloned.1.call-update) | async-done | bytes 524304 | tf_op jit(solution)/shard_map/reduce_scatter | solution.py:169
  382.4 23.5 %reduce-scatter.8.cloned.1.call-done = bf16[32,2048]{1,0:T(8,128)(2,1)} async-done(((bf16[128,2048]{1,0:T(8,128)(2,1)}), bf16[32,2048]{1,0:T(8,128)(2,1)}) %reduce-scatter.8.cloned.1.call-update) | async-done | bytes 131088 | tf_op jit(solution)/shard_map/reduce_scatter | solution.py:170
  (89 shorter events, 26.8 us)
Async XLA Ops:
  6.5 55.3 %copy-start = (bf16[2,4096,128]{2,1,0:T(8,128)(2,1)S(1)}, bf16[2,4096,128]{2,1,0:T(8,128)(2,1)}, u32[]{:S(2)}) copy-start(bf16[2,4096,128]{2,1,0:T(8,128)(2,1)} %param.24) | copy-start | bytes 6291460
  6.5 171.5 %all-reduce.5.cloned.1.call-start = ((), (), s32[]{:S(2)}) async-start(), calls=%async_computation.3 | async-start | bytes 2359296 | tf_op jit(solution)/shard_map/psum | solution.py:133
  23.7 4.0 copy-start.3
  23.7 4.0 copy-start.9
  23.7 4.0 copy-start.11
  27.7 1.0 copy-start.10
  75.0 1.3 copy-start.6
  80.9 18.1 %copy-start.12 = (bf16[128]{0:T(256)(128)(2,1)S(1)}, bf16[128]{0:T(256)(128)(2,1)}, u32[]{:S(2)}) copy-start(bf16[128]{0:T(256)(128)(2,1)} %constant.77.clone.1) | copy-start | bytes 772
  122.0 2.2 copy-start.2
  130.6 96.6 %reduce-scatter.4.cloned.1.call-start = ((), (), s32[]{:S(2)}) async-start(), calls=%async_computation.4 | async-start | bytes 1179648 | tf_op jit(solution)/shard_map/reduce_scatter | solution.py:145
  179.2 5.1 %copy-start.4 = (bf16[256,2048]{1,0:T(8,128)(2,1)S(1)}, bf16[256,2048]{1,0:T(8,128)(2,1)}, u32[]{:S(2)}) copy-start(bf16[256,2048]{1,0:T(8,128)(2,1)} %param.18) | copy-start | bytes 3145732
  184.3 54.6 %copy-start.5 = (f32[2048]{0:T(1024)S(1)}, f32[2048]{0:T(1024)}, u32[]{:S(2)}) copy-start(f32[2048]{0:T(1024)} %param.30) | copy-start | bytes 24580
  184.3 95.1 %all-gather.2.cloned.1.call-start = ((), (), s32[]{:S(2)}) async-start(), calls=%async_computation.5 | async-start | bytes 2621440 | tf_op jit(solution)/shard_map/all_gather | solution.py:159
  252.5 92.3 %all-reduce.7.cloned.1.call-start = ((), (), s32[]{:S(2)}) async-start(), calls=%async_computation.6 | async-start | bytes 3670016 | tf_op jit(solution)/shard_map/psum | solution.py:164
  252.6 4.1 collective-permute-start.1
  252.7 31.9 %collective-permute-start = (bf16[2048,448]{0,1:T(8,128)(2,1)}, bf16[2048,448]{0,1:T(8,128)(2,1)}, u32[]{:S(2)}, u32[]{:S(2)}) collective-permute-start(bf16[2048,448]{0,1:T(8,128)(2,1)} %param.31), channel_id=1, source_target_pairs={{0,32},{32,0},{1,33},{33,1},{2,34},{34,2},{3,35},{35,3},{4,36},{36... | collective-permute-start | bytes 5505032 | tf_op jit(solution)/shard_map/ppermute | solution.py:155
  256.6 1.3 copy-start.8
  279.3 5.2 %copy-start.7 = (bf16[512,2048]{1,0:T(8,128)(2,1)S(1)}, bf16[512,2048]{1,0:T(8,128)(2,1)}, u32[]{:S(2)}) copy-start(bf16[512,2048]{1,0:T(8,128)(2,1)} %all-gather.2.cloned.1.call-done) | copy-start | bytes 6291460
  290.4 92.0 %reduce-scatter.6.cloned.1.call-start = ((), (), s32[]{:S(2)}) async-start(), calls=%async_computation.7 | async-start | bytes 2621440 | tf_op jit(solution)/shard_map/reduce_scatter | solution.py:169
  290.4 56.1 %collective-permute-start.2 = (bf16[448,2048]{1,0:T(8,128)(2,1)}, bf16[448,2048]{1,0:T(8,128)(2,1)}, u32[]{:S(2)}, u32[]{:S(2)}) collective-permute-start(bf16[448,2048]{1,0:T(8,128)(2,1)} %param.33), channel_id=1, source_target_pairs={{0,32},{32,0},{1,33},{33,1},{2,34},{34,2},{3,35},{35,3},{4,36},{36... | collective-permute-start | bytes 5505032 | tf_op jit(solution)/shard_map/ppermute | solution.py:157
  346.6 60.9 %copy-start.1 = (bf16[2,4096,128]{2,1,0:T(8,128)(2,1)S(1)}, bf16[2,4096,128]{2,1,0:T(8,128)(2,1)}, u32[]{:S(2)}) copy-start(bf16[2,4096,128]{2,1,0:T(8,128)(2,1)} %param.24) | copy-start | bytes 6291460
  352.6 53.3 %reduce-scatter.8.cloned.1.call-start = ((), (), s32[]{:S(2)}) async-start(), calls=%async_computation.8 | async-start | bytes 655360 | tf_op jit(solution)/shard_map/reduce_scatter | solution.py:170
Sparse Core Ops, SparseCore 0:
  130.7 47.2 all-reduce.4
  184.4 42.7 reduce-scatter.3
  252.6 26.6 all-gather.1
  290.5 54.2 all-reduce.6
  352.7 29.6 reduce-scatter.5
  384.6 21.1 reduce-scatter.7

commit v6 on v4

--- a/solution.py
+++ b/solution.py
@@ -32,6 +32,25 @@
     total = total_one * scale_one + total_two * scale_two
     numer = numer_one * scale_one[..., None] + numer_two * scale_two[..., None]
     return (peak, total, numer)
+
+
+def pair_gather(part, axis):
+    swap = [(0, 1), (1, 0)]
+    other = lax.ppermute(part, axis, swap)
+    first = lax.axis_index(axis) == 0
+    return jnp.where(
+        first, jnp.concatenate([part, other], axis=0), jnp.concatenate([other, part], axis=0)
+    )
+
+
+def pair_reduce(rows, axis):
+    swap = [(0, 1), (1, 0)]
+    index = lax.axis_index(axis)
+    halves = rows.reshape((2, rows.shape[0] // 2) + rows.shape[1:])
+    mine = lax.dynamic_index_in_dim(halves, index, 0, keepdims=False)
+    other = lax.dynamic_index_in_dim(halves, 1 - index, 0, keepdims=False)
+    other = lax.ppermute(other.astype(jnp.bfloat16), axis, swap)
+    return mine.astype(jnp.float32) + other.astype(jnp.float32)
 
 
 def body(
@@ -149,8 +168,9 @@
     share = stream_count // (lax.axis_size("z") * lax.axis_size("xlo"))
     tp_start = (lax.axis_index("z") * lax.axis_size("xlo") + lax.axis_index("xlo")) * share
     summed = lax.psum_scatter(
-        partial_out.astype(jnp.bfloat16), TP, scatter_dimension=0, tiled=True
-    )
+        partial_out.astype(jnp.bfloat16), "z", scatter_dimension=0, tiled=True
+    )
+    summed = pair_reduce(summed, "xlo")
     own_hidden = lax.dynamic_slice_in_dim(hidden_float, tp_start, share, 0)
     middle = (own_hidden + summed.astype(jnp.float32)).astype(jnp.bfloat16)
     middle_float = middle.astype(jnp.float32)
@@ -161,7 +181,7 @@
     gate_both = jnp.concatenate([w_gate, lax.ppermute(w_gate, "core", swap)], axis=1)
     up_both = jnp.concatenate([w_up, lax.ppermute(w_up, "core", swap)], axis=1)
     down_both = jnp.concatenate([w_down, lax.ppermute(w_down, "core", swap)], axis=0)
-    normed_row = lax.all_gather(normed_own, ("hi", "xlo"), axis=0, tiled=True)
+    normed_row = pair_gather(pair_gather(normed_own, "xlo"), "hi")
     normed_half = lax.all_gather(normed_row, "z", axis=0, tiled=True)
     hidden_units = gate_both.shape[1]
     part_gate = jnp.dot(normed_half, gate_both, preferred_element_type=jnp.float32)
@@ -174,7 +194,7 @@
     act_all = lax.all_gather(act, "grp", axis=0, tiled=True)
     down = jnp.dot(act_all, down_both, preferred_element_type=jnp.float32)
     returned = lax.psum_scatter(down.astype(jnp.bfloat16), "z", scatter_dimension=0, tiled=True)
-    returned = lax.psum_scatter(returned, ("hi", "xlo"), scatter_dimension=0, tiled=True)
+    returned = pair_reduce(pair_reduce(returned, "hi").astype(jnp.bfloat16), "xlo")
     return (middle_float + returned.astype(jnp.float32)).astype(jnp.bfloat16)
 
 

time: 391 us -> 375 us (0.959)
  waiting for transfers between devices: 170 us -> 154 us
  blocking collectives: 110 us -> 96.7 us
  starting transfers between devices: 0.88 us -> 11.6 us
    reduce_scatter x2 -> x1, waiting for transfers between devices: 63.5 us -> 23.7 us  [body(): lax.psum_scatter(partial_out.astype(jnp.bfloat16), 'z', scatter_dimension...]
    ppermute x0 -> x5, waiting for transfers between devices: none -> 21.7 us  [the longest x3 11.9 us: pair_reduce(): other = lax.ppermute(other.astype(jnp.bfloat16), axis, swap)]
    all_gather x1 -> x0, blocking collectives: 13.5 us -> none  [body(): normed_row = lax.all_gather(normed_own, ('hi', 'xlo'), axis=0, tiled=True)]
    ppermute x0 -> x5, starting transfers between devices: none -> 10.7 us  [the longest x3 6.21 us: pair_reduce(): other = lax.ppermute(other.astype(jnp.bfloat16), axis, swap)]
  transfers between devices with their start and end apart: 9 -> 13, of which waited for: 7 -> 11; matrix products, arithmetic and copies ran while one was open for 2% -> 2% of each run, Pallas kernels for 0% -> 0%
where the time goes in v6:
time: 375 us; the launch traced here: 374 us
  waiting for transfers between devices  154 us (41%)
  blocking collectives  96.7 us (26%)
  matrix products  61.5 us (16%)
  local copies, waits for them, and re-layouts  20.1 us (5%)
  other arithmetic  16.7 us (4%)
  between operations  13.5 us (4%)
  starting transfers between devices  11.6 us (3%)
    psum x1, blocking collectives, body(): lax.psum((part_query, part_key, part_value), 'grp')  30.7 us
    reduce_scatter x1, waiting for transfers between devices, body(): lax.psum_scatter(down.astype(jnp.bfloat16), 'z', scatter_dimension=0, til...  29.8 us
    reduce_scatter x1, waiting for transfers between devices, body(): lax.psum_scatter(both, 'grp', scatter_dimension=0, tiled=True)  27.4 us
    reduce_scatter x1, waiting for transfers between devices, body(): reduced = lax.psum_scatter(packed, 'grp', scatter_dimension=0, tiled=True)  24.8 us
    reduce_scatter x1, waiting for transfers between devices, body(): lax.psum_scatter(partial_out.astype(jnp.bfloat16), 'z', scatter_dimension...  23.7 us
    all_gather x1, waiting for transfers between devices, body(): normed_half = lax.all_gather(normed_row, 'z', axis=0, tiled=True)  23.1 us
    pmax x1, blocking collectives, body(): lax.pmax(jnp.maximum(jnp.maximum(pre_peak, suf_scores.max(axis=3)), own_s...  17.3 us
    dot_general x1, matrix products, body(): jnp.einsum('pskgj,pjkd->pskgd', pre_weights, pre_value_ext, preferred_ele...  15.1 us
  transfers between devices with their start and end apart: 13, of which 11 were waited for; matrix products, arithmetic and copies ran while one was open for 2% of the time, Pallas kernels for 0%

profile of v6, /device:TPU:0, one launch (start us, length us, event | category | flops | bytes accessed | tf_op | source)
XLA Modules:
  0.0 374.3 jit_solution(11682471747861872785)
XLA Ops:
  12.8 10.9 %psum.35 = f32[256]{0:T(256)S(1)} all-reduce(f32[256]{0:T(256)S(1)} %multiply_reduce_fusion), channel_id=1, replica_groups=mesh['hi'=2,'core'=2,'grp'=4,'z'=4,'xlo'=2] {'grp'}, use_global_device_ids=true, to_apply=%region_1.0 | all-reduce | flops 256 | bytes 2048 | tf_op jit(solution)/shard_map/psum | solution.py:76
  23.7 3.9 %fusion.63 = f32[256,1024]{1,0:T(8,128)S(1)} fusion(bf16[2048,1024]{1,0:T(8,128)(2,1)} %param.20, f32[2048]{0:T(1024)} %param.19, f32[256]{0:T(256)S(1)} %add_rsqrt_fusion, bf16[256,2048]{1,0:T(8,128)(2,1)} %param.18), kind=kOutput, calls=%fused_computation.111 | convolution fusion | flops 1075838976 | bytes 6300672 | tf_op jit(solution)/shard_map/dot_general | solution.py:79
  29.2 30.7 %all-reduce.2 = (bf16[256,1024]{1,0:T(8,128)(2,1)}, bf16[256,128]{1,0:T(8,128)(2,1)S(1)}, bf16[256,128]{1,0:T(8,128)(2,1)S(1)}) all-reduce(f32[256,1024]{1,0:T(8,128)S(1)} %fusion.63, f32[256,128]{1,0:T(8,128)S(1)} %fusion.62, f32[256,128]{1,0:T(8,128)S(1)} %fusion.61), channel_id=1, replica_groups=mesh['hi'=2,'core'=2,'grp'=4,'z'=4,'xlo'=2] {'grp'}, use_global_device_ids=true, to_apply=%region_2.0 | all-reduce | flops 327680 | bytes 1966080 | tf_op jit(solution)/shard_map/psum | solution.py:82
  61.9 13.1 %bitcast_reduce_fusion = (f32[2,128,8]{1,2,0:T(8,128)S(1)}, f32[2,128,8,4096]{3,1,2,0:T(8,128)}) fusion(bf16[2,4096,128]{2,1,0:T(8,128)(2,1)S(1)} %copy-done, bf16[2,128,8,128]{3,2,1,0:T(8,128)(2,1)S(1)} %bitcast.152), kind=kOutput, calls=%fused_computation.6 | convolution fusion | flops 2164258816 | bytes 36184064 | tf_op jit(solution)/shard_map/pskgd,pjkd->pskgj/dot_general | solution.py:113
  76.4 4.5 %fusion.66 = (f32[256,8]{1,0:T(8,128)S(1)}, f32[256,8,64]{2,1,0:T(8,128)S(1)}) fusion(bf16[256,8,128]{2,1,0:T(8,128)(2,1)S(1)} %bitcast.149, bf16[256,64,128]{2,1,0:T(8,128)(2,1)} %param.26, pred[256,64]{1,0:T(8,128)(4,1)S(1)} %broadcast_compare_fusion), kind=kOutput, calls=%fused_computation.112 | convolution fusion | flops 33945600 | bytes 5267456 | tf_op jit(solution)/shard_map/skgd,sjkd->skgj/dot_general | solution.py:120
  81.0 17.3 %pmax.7 = f32[256,1,8]{2,0,1:T(8,128)S(1)} all-reduce(f32[256,1,8]{2,0,1:T(8,128)S(1)} %get-tuple-element.25), channel_id=1, replica_groups=mesh['hi'=2,'core'=2,'grp'=4,'z'=4,'xlo'=2] {'grp'}, use_global_device_ids=true, to_apply=%region_10.11 | all-reduce | flops 2048 | bytes 16384 | tf_op jit(solution)/shard_map/pmax | solution.py:132
  99.1 15.1 %fusion.26 = f32[2,128,1,8,256]{4,1,3,0,2:T(8,128)} fusion(f32[2,128,8,4096]{3,1,2,0:T(8,128)} %get-tuple-element.27, f32[2,128,8]{1,2,0:T(8,128)S(1)} %copy.26, bf16[2,4096,1,128]{3,1,0,2:T(8,128)(2,1)} %bitcast.165, bf16[256]{0:T(256)(128)(2,1)S(1)} %pad.21.clone), kind=kOutput, calls=%fused_computation.35 | convolution fusion | flops 4328521728 | bytes 37757440 | tf_op jit(solution)/shard_map/pskgj,pjkd->pskgd/dot_general | solution.py:139
  114.2 4.2 %copy.27 = f32[2,128,1,8,256]{4,3,1,0,2:T(8,128)} copy(f32[2,128,1,8,256]{4,1,3,0,2:T(8,128)} %fusion.26) | data formatting | bytes 4194304 | tf_op jit(solution)/shard_map/pskgj,pjkd->pskgd/transpose | solution.py:139
  118.4 3.6 gather_fusion.3
  130.8 24.8 %reduce-scatter.5.cloned.1.call-done = f32[64,1032]{1,0:T(8,128)} async-done(((f32[256,1032]{1,0:T(8,128)}), f32[64,1032]{1,0:T(8,128)}) %reduce-scatter.5.cloned.1.call-update) | async-done | bytes 264208 | tf_op jit(solution)/shard_map/reduce_scatter | solution.py:152
  157.6 12.8 %all_gather.9 = bf16[256,1024]{1,0:T(8,128)(2,1)S(1)} all-gather(bf16[64,1024]{1,0:T(8,128)(2,1)S(1)} %fusion.44), channel_id=1, replica_groups=mesh['hi'=2,'core'=2,'grp'=4,'z'=4,'xlo'=2] {'grp'}, dimensions={0}, use_global_device_ids=true | all-gather | bytes 655360 | tf_op jit(solution)/shard_map/all_gather | solution.py:166
  170.4 4.5 %convolution_convert_fusion = bf16[256,2048]{1,0:T(8,128)(2,1)} fusion(bf16[256,1024]{1,0:T(8,128)(2,1)S(1)} %all_gather.9, bf16[1024,2048]{1,0:T(8,128)(2,1)} %param.23), kind=kOutput, calls=%fused_computation.28 | convolution fusion | flops 1074266112 | bytes 5767168 | tf_op jit(solution)/shard_map/dot_general | solution.py:167
  175.0 23.7 %reduce-scatter.7.cloned.1.call-done = bf16[64,2048]{1,0:T(8,128)(2,1)} async-done(((bf16[256,2048]{1,0:T(8,128)(2,1)}), bf16[64,2048]{1,0:T(8,128)(2,1)}) %reduce-scatter.7.cloned.1.call-update) | async-done | bytes 262160 | tf_op jit(solution)/shard_map/reduce_scatter | solution.py:170
  205.9 10.5 %psum.39 = f32[32]{0:T(128)S(1)} all-reduce(f32[32]{0:T(128)S(1)} %get-tuple-element.20), channel_id=1, replica_groups=mesh['hi'=2,'core'=2,'grp'=4,'z'=4,'xlo'=2] {'grp'}, use_global_device_ids=true, to_apply=%region_16.17 | all-reduce | flops 32 | bytes 256 | tf_op jit(solution)/shard_map/psum | solution.py:177
  218.0 4.9 %collective-permute-done.1 = bf16[32,2048]{1,0:T(8,128)(2,1)S(1)} collective-permute-done((bf16[32,2048]{1,0:T(8,128)(2,1)S(1)}, bf16[32,2048]{1,0:T(8,128)(2,1)S(1)}, u32[]{:S(2)}, u32[]{:S(2)}) %collective-permute-start.1) | collective-permute-done | bytes 131104 | tf_op jit(solution)/shard_map/ppermute | solution.py:39
  226.0 5.0 %collective-permute-done.2 = bf16[64,2048]{1,0:T(8,128)(2,1)S(1)} collective-permute-done((bf16[64,2048]{1,0:T(8,128)(2,1)S(1)}, bf16[64,2048]{1,0:T(8,128)(2,1)S(1)}, u32[]{:S(2)}, u32[]{:S(2)}) %collective-permute-start.2) | collective-permute-done | bytes 262176 | tf_op jit(solution)/shard_map/ppermute | solution.py:39
  237.3 23.1 %all-gather.2.cloned.1.call-done = bf16[512,2048]{1,0:T(8,128)(2,1)} async-done(((bf16[128,2048]{1,0:T(8,128)(2,1)}), bf16[512,2048]{1,0:T(8,128)(2,1)}) %all-gather.2.cloned.1.call-update) | async-done | bytes 2097168 | tf_op jit(solution)/shard_map/all_gather | solution.py:185
  260.4 5.2 %fusion.29 = bf16[512,896]{1,0:T(8,128)(2,1)S(1)} fusion(bf16[512,2048]{1,0:T(8,128)(2,1)} %all-gather.2.cloned.1.call-done, bf16[2048,448]{0,1:T(8,128)(2,1)} %copy-done.9, bf16[2048,448]{0,1:T(8,128)(2,1)} %param.32), kind=kOutput, calls=%fused_computation.36 | convolution fusion | flops 1886846976 | bytes 6684672 | tf_op jit(solution)/shard_map/dot_general | solution.py:188
  265.7 4.4 %fusion.32 = bf16[512,896]{1,0:T(8,128)(2,1)S(1)} fusion(bf16[512,2048]{1,0:T(8,128)(2,1)S(1)} %copy-done.8, bf16[2048,448]{0,1:T(8,128)(2,1)} %collective-permute-done.3, bf16[2048,448]{0,1:T(8,128)(2,1)} %param.31), kind=kOutput, calls=%fused_computation.37 | convolution fusion | flops 1886846976 | bytes 6684672 | tf_op jit(solution)/shard_map/dot_general | solution.py:187
  271.6 27.4 %reduce-scatter.9.cloned.1.call-done = bf16[128,1792]{1,0:T(8,128)(2,1)} async-done(((bf16[512,1792]{1,0:T(8,128)(2,1)}), bf16[128,1792]{1,0:T(8,128)(2,1)}) %reduce-scatter.9.cloned.1.call-update) | async-done | bytes 458768 | tf_op jit(solution)/shard_map/reduce_scatter | solution.py:190
  300.3 14.6 %all_gather.11 = bf16[512,896]{1,0:T(8,128)(2,1)S(1)} all-gather(bf16[128,896]{1,0:T(8,128)(2,1)S(1)} %fusion.39), channel_id=1, replica_groups=mesh['hi'=2,'core'=2,'grp'=4,'z'=4,'xlo'=2] {'grp'}, dimensions={0}, use_global_device_ids=true | all-gather | bytes 1146880 | tf_op jit(solution)/shard_map/all_gather | solution.py:194
  314.9 5.7 %fusion.20 = bf16[512,2048]{1,0:T(8,128)(2,1)} fusion(bf16[512,896]{1,0:T(8,128)(2,1)S(1)} %all_gather.11, bf16[448,2048]{1,0:T(8,128)(2,1)} %collective-permute-done.5, bf16[448,2048]{1,0:T(8,128)(2,1)} %param.33), kind=kOutput, calls=%fused_computation.27 | convolution fusion | flops 1887436800 | bytes 6684672 | tf_op jit(solution)/shard_map/dot_general | solution.py:195
  320.7 29.8 %reduce-scatter.11.cloned.1.call-done = bf16[128,2048]{1,0:T(8,128)(2,1)} async-done(((bf16[512,2048]{1,0:T(8,128)(2,1)}), bf16[128,2048]{1,0:T(8,128)(2,1)}) %reduce-scatter.11.cloned.1.call-update) | async-done | bytes 524304 | tf_op jit(solution)/shard_map/reduce_scatter | solution.py:196
  354.5 6.5 %collective-permute-done.6 = bf16[64,2048]{1,0:T(8,128)(2,1)S(1)} collective-permute-done((bf16[64,2048]{1,0:T(8,128)(2,1)S(1)}, bf16[64,2048]{1,0:T(8,128)(2,1)S(1)}, u32[]{:S(2)}, u32[]{:S(2)}) %collective-permute-start.6) | collective-permute-done | bytes 262176 | tf_op jit(solution)/shard_map/ppermute | solution.py:52
  (107 shorter events, 54.4 us)
Async XLA Ops:
  6.5 55.3 %copy-start = (bf16[2,4096,128]{2,1,0:T(8,128)(2,1)S(1)}, bf16[2,4096,128]{2,1,0:T(8,128)(2,1)}, u32[]{:S(2)}) copy-start(bf16[2,4096,128]{2,1,0:T(8,128)(2,1)} %param.24) | copy-start | bytes 6291460
  6.5 149.1 %reduce-scatter.5.cloned.1.call-start = ((), (), s32[]{:S(2)}) async-start(), calls=%async_computation.4 | async-start | bytes 1474560 | tf_op jit(solution)/shard_map/reduce_scatter | solution.py:152
  23.7 4.0 %copy-start.3 = (bf16[256,2048]{1,0:T(8,128)(2,1)S(1)}, bf16[256,2048]{1,0:T(8,128)(2,1)}, u32[]{:S(2)}) copy-start(bf16[256,2048]{1,0:T(8,128)(2,1)} %param.18) | copy-start | bytes 3145732
  23.7 4.0 %copy-start.10 = (bf16[2048,128]{1,0:T(8,128)(2,1)S(1)}, bf16[2048,128]{1,0:T(8,128)(2,1)}, u32[]{:S(2)}) copy-start(bf16[2048,128]{1,0:T(8,128)(2,1)} %param.22) | copy-start | bytes 1572868
  23.7 4.0 %copy-start.12 = (f32[2048]{0:T(1024)S(1)}, f32[2048]{0:T(1024)}, u32[]{:S(2)}) copy-start(f32[2048]{0:T(1024)} %param.19) | copy-start | bytes 24580
  80.9 18.1 %copy-start.13 = (bf16[128]{0:T(256)(128)(2,1)S(1)}, bf16[128]{0:T(256)(128)(2,1)}, u32[]{:S(2)}) copy-start(bf16[128]{0:T(256)(128)(2,1)} %constant.96.clone.1) | copy-start | bytes 772
  122.0 2.2 copy-start.2
  130.6 68.1 %reduce-scatter.7.cloned.1.call-start = ((), (), s32[]{:S(2)}) async-start(), calls=%async_computation.5 | async-start | bytes 1310720 | tf_op jit(solution)/shard_map/reduce_scatter | solution.py:170
  170.3 30.9 %copy-start.4 = (bf16[256,2048]{1,0:T(8,128)(2,1)S(1)}, bf16[256,2048]{1,0:T(8,128)(2,1)}, u32[]{:S(2)}) copy-start(bf16[256,2048]{1,0:T(8,128)(2,1)} %param.18) | copy-start | bytes 3145732
  174.9 41.5 %copy-start.6 = (f32[2048]{0:T(1024)S(1)}, f32[2048]{0:T(1024)}, u32[]{:S(2)}) copy-start(f32[2048]{0:T(1024)} %param.30) | copy-start | bytes 24580
  174.9 85.5 %all-gather.2.cloned.1.call-start = ((), (), s32[]{:S(2)}) async-start(), calls=%async_computation.6 | async-start | bytes 2621440 | tf_op jit(solution)/shard_map/all_gather | solution.py:185
  198.7 6.0 %copy-start.5 = (bf16[64,2048]{1,0:T(8,128)(2,1)S(1)}, bf16[64,2048]{1,0:T(8,128)(2,1)}, u32[]{:S(2)}) copy-start(bf16[64,2048]{1,0:T(8,128)(2,1)} %reduce-scatter.7.cloned.1.call-done) | copy-start | bytes 786436
  199.7 5.0 %collective-permute-start = (bf16[32,2048]{1,0:T(8,128)(2,1)S(1)}, bf16[32,2048]{1,0:T(8,128)(2,1)S(1)}, u32[]{:S(2)}, u32[]{:S(2)}) collective-permute-start(bf16[32,2048]{1,0:T(8,128)(2,1)S(1)} %dynamic-slice_bitcast_fusion.2), channel_id=1, source_target_pairs={{0,1},{1,0},{2,3},{3,2},{4,5},{5,4},{6,7},{7,6},{8,9},{9,8},{10,11... | collective-permute-start | bytes 393224 | tf_op jit(solution)/shard_map/ppermute | solution.py:52
  216.5 6.4 %collective-permute-start.1 = (bf16[32,2048]{1,0:T(8,128)(2,1)S(1)}, bf16[32,2048]{1,0:T(8,128)(2,1)S(1)}, u32[]{:S(2)}, u32[]{:S(2)}) collective-permute-start(bf16[32,2048]{1,0:T(8,128)(2,1)S(1)} %fusion.42), channel_id=1, source_target_pairs={{0,1},{1,0},{2,3},{3,2},{4,5},{5,4},{6,7},{7,6},{8,9},{9,8},{10,11... | collective-permute-start | bytes 393224 | tf_op jit(solution)/shard_map/ppermute | solution.py:39
  223.0 8.0 %collective-permute-start.2 = (bf16[64,2048]{1,0:T(8,128)(2,1)S(1)}, bf16[64,2048]{1,0:T(8,128)(2,1)S(1)}, u32[]{:S(2)}, u32[]{:S(2)}) collective-permute-start(bf16[64,2048]{1,0:T(8,128)(2,1)S(1)} %maximum_select_fusion.1), channel_id=1, source_target_pairs={{0,64},{64,0},{1,65},{65,1},{2,66},{66,2},{3,67},{67,3},{4,68},{68... | collective-permute-start | bytes 786440 | tf_op jit(solution)/shard_map/ppermute | solution.py:39
  231.9 67.2 %reduce-scatter.9.cloned.1.call-start = ((), (), s32[]{:S(2)}) async-start(), calls=%async_computation.7 | async-start | bytes 2293760 | tf_op jit(solution)/shard_map/reduce_scatter | solution.py:190
  232.0 4.1 %collective-permute-start.4 = (bf16[2048,448]{0,1:T(8,128)(2,1)}, bf16[2048,448]{0,1:T(8,128)(2,1)S(1)}, u32[]{:S(2)}, u32[]{:S(2)}) collective-permute-start(bf16[2048,448]{0,1:T(8,128)(2,1)} %param.32), channel_id=1, source_target_pairs={{0,32},{32,0},{1,33},{33,1},{2,34},{34,2},{3,35},{35,3},{4,36},{36... | collective-permute-start | bytes 5505032 | tf_op jit(solution)/shard_map/ppermute | solution.py:182
  232.1 33.6 %collective-permute-start.3 = (bf16[2048,448]{0,1:T(8,128)(2,1)}, bf16[2048,448]{0,1:T(8,128)(2,1)}, u32[]{:S(2)}, u32[]{:S(2)}) collective-permute-start(bf16[2048,448]{0,1:T(8,128)(2,1)} %param.31), channel_id=1, source_target_pairs={{0,32},{32,0},{1,33},{33,1},{2,34},{34,2},{3,35},{35,3},{4,36},{36... | collective-permute-start | bytes 5505032 | tf_op jit(solution)/shard_map/ppermute | solution.py:181
  260.4 5.2 %copy-start.8 = (bf16[512,2048]{1,0:T(8,128)(2,1)S(1)}, bf16[512,2048]{1,0:T(8,128)(2,1)}, u32[]{:S(2)}) copy-start(bf16[512,2048]{1,0:T(8,128)(2,1)} %all-gather.2.cloned.1.call-done) | copy-start | bytes 6291460
  271.5 78.9 %reduce-scatter.11.cloned.1.call-start = ((), (), s32[]{:S(2)}) async-start(), calls=%async_computation.8 | async-start | bytes 2621440 | tf_op jit(solution)/shard_map/reduce_scatter | solution.py:196
  271.5 43.3 %collective-permute-start.5 = (bf16[448,2048]{1,0:T(8,128)(2,1)}, bf16[448,2048]{1,0:T(8,128)(2,1)}, u32[]{:S(2)}, u32[]{:S(2)}) collective-permute-start(bf16[448,2048]{1,0:T(8,128)(2,1)} %param.33), channel_id=1, source_target_pairs={{0,32},{32,0},{1,33},{33,1},{2,34},{34,2},{3,35},{35,3},{4,36},{36... | collective-permute-start | bytes 5505032 | tf_op jit(solution)/shard_map/ppermute | solution.py:183
  320.6 47.2 %copy-start.1 = (bf16[2,4096,128]{2,1,0:T(8,128)(2,1)S(1)}, bf16[2,4096,128]{2,1,0:T(8,128)(2,1)}, u32[]{:S(2)}) copy-start(bf16[2,4096,128]{2,1,0:T(8,128)(2,1)} %param.24) | copy-start | bytes 6291460
  351.4 9.6 %collective-permute-start.6 = (bf16[64,2048]{1,0:T(8,128)(2,1)S(1)}, bf16[64,2048]{1,0:T(8,128)(2,1)S(1)}, u32[]{:S(2)}, u32[]{:S(2)}) collective-permute-start(bf16[64,2048]{1,0:T(8,128)(2,1)S(1)} %dynamic-slice_bitcast_fusion), channel_id=1, source_target_pairs={{0,64},{64,0},{1,65},{65,1},{2,66},{66,2},{3,67},{67,3},{4,68},{68... | collective-permute-start | bytes 786440 | tf_op jit(solution)/shard_map/ppermute | solution.py:52
  362.0 5.0 %collective-permute-start.7 = (bf16[32,2048]{1,0:T(8,128)(2,1)S(1)}, bf16[32,2048]{1,0:T(8,128)(2,1)S(1)}, u32[]{:S(2)}, u32[]{:S(2)}) collective-permute-start(bf16[32,2048]{1,0:T(8,128)(2,1)S(1)} %dynamic-slice_bitcast_fusion.1), channel_id=1, source_target_pairs={{0,1},{1,0},{2,3},{3,2},{4,5},{5,4},{6,7},{7,6},{8,9},{9,8},{10,11... | collective-permute-start | bytes 393224 | tf_op jit(solution)/shard_map/ppermute | solution.py:52
  (3 other events, 3.6 us)
Sparse Core Ops, SparseCore 0:
  130.7 24.8 reduce-scatter.4
  175.0 23.6 reduce-scatter.6
  232.0 28.3 all-gather.1
  271.6 27.4 reduce-scatter.8
  320.8 29.6 reduce-scatter.10

commit v7 on v6

--- a/solution.py
+++ b/solution.py
@@ -51,6 +51,30 @@
     other = lax.dynamic_index_in_dim(halves, 1 - index, 0, keepdims=False)
     other = lax.ppermute(other.astype(jnp.bfloat16), axis, swap)
     return mine.astype(jnp.float32) + other.astype(jnp.float32)
+
+
+def ring_gather(part, axis):
+    size = lax.axis_size(axis)
+    index = lax.axis_index(axis)
+    pieces = [part]
+    for shift in range(1, size):
+        pairs = [(i, (i + shift) % size) for i in range(size)]
+        pieces.append(lax.ppermute(part, axis, pairs))
+    stacked = jnp.stack(pieces)
+    order = (index - jnp.arange(size, dtype=jnp.int32)) % size
+    return stacked[order].reshape((size * part.shape[0],) + part.shape[1:])
+
+
+def ring_reduce(rows, axis):
+    size = lax.axis_size(axis)
+    index = lax.axis_index(axis)
+    blocks = rows.reshape((size, rows.shape[0] // size) + rows.shape[1:])
+    total = lax.dynamic_index_in_dim(blocks, index, 0, keepdims=False).astype(jnp.float32)
+    for shift in range(1, size):
+        pairs = [(i, (i + shift) % size) for i in range(size)]
+        outgoing = lax.dynamic_index_in_dim(blocks, (index + shift) % size, 0, keepdims=False)
+        total = total + lax.ppermute(outgoing, axis, pairs).astype(jnp.float32)
+    return total
 
 
 def body(
@@ -167,9 +191,7 @@
     partial_out = jnp.dot(attended, w_out, preferred_element_type=jnp.float32)
     share = stream_count // (lax.axis_size("z") * lax.axis_size("xlo"))
     tp_start = (lax.axis_index("z") * lax.axis_size("xlo") + lax.axis_index("xlo")) * share
-    summed = lax.psum_scatter(
-        partial_out.astype(jnp.bfloat16), "z", scatter_dimension=0, tiled=True
-    )
+    summed = ring_reduce(partial_out.astype(jnp.bfloat16), "z")
     summed = pair_reduce(summed, "xlo")
     own_hidden = lax.dynamic_slice_in_dim(hidden_float, tp_start, share, 0)
     middle = (own_hidden + summed.astype(jnp.float32)).astype(jnp.bfloat16)
@@ -182,7 +204,7 @@
     up_both = jnp.concatenate([w_up, lax.ppermute(w_up, "core", swap)], axis=1)
     down_both = jnp.concatenate([w_down, lax.ppermute(w_down, "core", swap)], axis=0)
     normed_row = pair_gather(pair_gather(normed_own, "xlo"), "hi")
-    normed_half = lax.all_gather(normed_row, "z", axis=0, tiled=True)
+    normed_half = ring_gather(normed_row, "z")
     hidden_units = gate_both.shape[1]
     part_gate = jnp.dot(normed_half, gate_both, preferred_element_type=jnp.float32)
     part_upward = jnp.dot(normed_half, up_both, preferred_element_type=jnp.float32)
@@ -193,7 +215,7 @@
     act = (jax.nn.silu(gate) * upward).astype(jnp.bfloat16)
     act_all = lax.all_gather(act, "grp", axis=0, tiled=True)
     down = jnp.dot(act_all, down_both, preferred_element_type=jnp.float32)
-    returned = lax.psum_scatter(down.astype(jnp.bfloat16), "z", scatter_dimension=0, tiled=True)
+    returned = ring_reduce(down.astype(jnp.bfloat16), "z").astype(jnp.bfloat16)
     returned = pair_reduce(pair_reduce(returned, "hi").astype(jnp.bfloat16), "xlo")
     return (middle_float + returned.astype(jnp.float32)).astype(jnp.bfloat16)
 

time: 375 us -> 348 us (0.928)
  waiting for transfers between devices: 154 us -> 112 us
  starting transfers between devices: 11.6 us -> 29.1 us
    reduce_scatter x2 -> x0, waiting for transfers between devices: 53.5 us -> none  [the longest x1 29.8 us: body(): lax.psum_scatter(down.astype(jnp.bfloat16), 'z', scatter_dimension=0, til...]
    ppermute x0 -> x9, waiting for transfers between devices: none -> 42.8 us  [the longest x6 25 us: ring_reduce(): total = total + lax.ppermute(outgoing, axis, pairs).astype(jnp.float32)]
    all_gather x1 -> x0, waiting for transfers between devices: 23.1 us -> none  [body(): normed_half = lax.all_gather(normed_row, 'z', axis=0, tiled=True)]
    ppermute x0 -> x9, starting transfers between devices: none -> 17.3 us  [the longest x6 11.7 us: ring_reduce(): total = total + lax.ppermute(outgoing, axis, pairs).astype(jnp.float32)]
  transfers between devices with their start and end apart: 13 -> 19, of which waited for: 11 -> 13; matrix products, arithmetic and copies ran while one was open for 2% -> 3% of each run, Pallas kernels for 0% -> 0%
where the time goes in v7:
time: 348 us; the launch traced here: 347 us
  waiting for transfers between devices  112 us (32%)
  blocking collectives  94.1 us (27%)
  matrix products  58.5 us (17%)
  starting transfers between devices  29.1 us (8%)
  local copies, waits for them, and re-layouts  21.4 us (6%)
  other arithmetic  18.2 us (5%)
  between operations  13.9 us (4%)
    psum x1, blocking collectives, body(): lax.psum((part_query, part_key, part_value), 'grp')  30.7 us
    reduce_scatter x1, waiting for transfers between devices, body(): lax.psum_scatter(both, 'grp', scatter_dimension=0, tiled=True)  26.3 us
    ppermute x6, waiting for transfers between devices, ring_reduce(): total = total + lax.ppermute(outgoing, axis, pairs).astype(jnp.float32)  25 us
    reduce_scatter x1, waiting for transfers between devices, body(): reduced = lax.psum_scatter(packed, 'grp', scatter_dimension=0, tiled=True)  24.7 us
    ppermute x3, waiting for transfers between devices, ring_gather(): pieces.append(lax.ppermute(part, axis, pairs))  17.8 us
    pmax x1, blocking collectives, body(): lax.pmax(jnp.maximum(jnp.maximum(pre_peak, suf_scores.max(axis=3)), own_s...  17.3 us
    dot_general x1, matrix products, body(): jnp.einsum('pskgj,pjkd->pskgd', pre_weights, pre_value_ext, preferred_ele...  15.1 us
    all_gather x1, blocking collectives, body(): act_all = lax.all_gather(act, 'grp', axis=0, tiled=True)  14.6 us
  transfers between devices with their start and end apart: 19, of which 13 were waited for; matrix products, arithmetic and copies ran while one was open for 3% of the time, Pallas kernels for 0%

profile of v7, /device:TPU:0, one launch (start us, length us, event | category | flops | bytes accessed | tf_op | source)
XLA Modules:
  0.0 347.0 jit_solution(5440654512804066479)
XLA Ops:
  12.8 10.9 %psum.35 = f32[256]{0:T(256)S(1)} all-reduce(f32[256]{0:T(256)S(1)} %multiply_reduce_fusion), channel_id=1, replica_groups=mesh['hi'=2,'core'=2,'grp'=4,'z'=4,'xlo'=2] {'grp'}, use_global_device_ids=true, to_apply=%region_1.0 | all-reduce | flops 256 | bytes 2048 | tf_op jit(solution)/shard_map/psum | solution.py:100
  23.7 3.9 %fusion.71 = f32[256,1024]{1,0:T(8,128)S(1)} fusion(bf16[2048,1024]{1,0:T(8,128)(2,1)} %param.20, f32[2048]{0:T(1024)} %param.19, f32[256]{0:T(256)S(1)} %add_rsqrt_fusion, bf16[256,2048]{1,0:T(8,128)(2,1)} %param.18), kind=kOutput, calls=%fused_computation.135 | convolution fusion | flops 1075838976 | bytes 6300672 | tf_op jit(solution)/shard_map/dot_general | solution.py:103
  29.2 30.7 %all-reduce.2 = (bf16[256,1024]{1,0:T(8,128)(2,1)}, bf16[256,128]{1,0:T(8,128)(2,1)S(1)}, bf16[256,128]{1,0:T(8,128)(2,1)S(1)}) all-reduce(f32[256,1024]{1,0:T(8,128)S(1)} %fusion.71, f32[256,128]{1,0:T(8,128)S(1)} %fusion.70, f32[256,128]{1,0:T(8,128)S(1)} %fusion.69), channel_id=1, replica_groups=mesh['hi'=2,'core'=2,'grp'=4,'z'=4,'xlo'=2] {'grp'}, use_global_device_ids=true, to_apply=%region_2.0 | all-reduce | flops 327680 | bytes 1966080 | tf_op jit(solution)/shard_map/psum | solution.py:106
  61.9 13.1 %bitcast_reduce_fusion = (f32[2,128,8]{1,2,0:T(8,128)S(1)}, f32[2,128,8,4096]{3,1,2,0:T(8,128)}) fusion(bf16[2,4096,128]{2,1,0:T(8,128)(2,1)S(1)} %copy-done, bf16[2,128,8,128]{3,2,1,0:T(8,128)(2,1)S(1)} %bitcast.183), kind=kOutput, calls=%fused_computation.7 | convolution fusion | flops 2164258816 | bytes 36184064 | tf_op jit(solution)/shard_map/pskgd,pjkd->pskgj/dot_general | solution.py:137
  76.4 4.5 %fusion.74 = (f32[256,8]{1,0:T(8,128)S(1)}, f32[256,8,64]{2,1,0:T(8,128)S(1)}) fusion(bf16[256,8,128]{2,1,0:T(8,128)(2,1)S(1)} %bitcast.180, bf16[256,64,128]{2,1,0:T(8,128)(2,1)} %param.26, pred[256,64]{1,0:T(8,128)(4,1)S(1)} %broadcast_compare_fusion), kind=kOutput, calls=%fused_computation.136 | convolution fusion | flops 33945600 | bytes 5267456 | tf_op jit(solution)/shard_map/skgd,sjkd->skgj/dot_general | solution.py:144
  81.0 17.3 %pmax.7 = f32[256,1,8]{2,0,1:T(8,128)S(1)} all-reduce(f32[256,1,8]{2,0,1:T(8,128)S(1)} %get-tuple-element.31), channel_id=1, replica_groups=mesh['hi'=2,'core'=2,'grp'=4,'z'=4,'xlo'=2] {'grp'}, use_global_device_ids=true, to_apply=%region_10.11 | all-reduce | flops 2048 | bytes 16384 | tf_op jit(solution)/shard_map/pmax | solution.py:156
  99.1 15.1 %fusion.26 = f32[2,128,1,8,256]{4,1,3,0,2:T(8,128)} fusion(f32[2,128,8,4096]{3,1,2,0:T(8,128)} %get-tuple-element.33, f32[2,128,8]{1,2,0:T(8,128)S(1)} %copy.26, bf16[2,4096,1,128]{3,1,0,2:T(8,128)(2,1)} %bitcast.207, bf16[256]{0:T(256)(128)(2,1)S(1)} %pad.29.clone), kind=kOutput, calls=%fused_computation.37 | convolution fusion | flops 4328521728 | bytes 37757440 | tf_op jit(solution)/shard_map/pskgj,pjkd->pskgd/dot_general | solution.py:163
  114.2 4.2 %copy.27 = f32[2,128,1,8,256]{4,3,1,0,2:T(8,128)} copy(f32[2,128,1,8,256]{4,1,3,0,2:T(8,128)} %fusion.26) | data formatting | bytes 4194304 | tf_op jit(solution)/shard_map/pskgj,pjkd->pskgd/transpose | solution.py:163
  130.9 24.7 %reduce-scatter.3.cloned.1.call-done = f32[64,1032]{1,0:T(8,128)} async-done(((f32[256,1032]{1,0:T(8,128)}), f32[64,1032]{1,0:T(8,128)}) %reduce-scatter.3.cloned.1.call-update) | async-done | bytes 264208 | tf_op jit(solution)/shard_map/reduce_scatter | solution.py:176
  157.5 12.8 %all_gather.6 = bf16[256,1024]{1,0:T(8,128)(2,1)S(1)} all-gather(bf16[64,1024]{1,0:T(8,128)(2,1)S(1)} %fusion.49), channel_id=1, replica_groups=mesh['hi'=2,'core'=2,'grp'=4,'z'=4,'xlo'=2] {'grp'}, dimensions={0}, use_global_device_ids=true | all-gather | bytes 655360 | tf_op jit(solution)/shard_map/all_gather | solution.py:190
  179.7 4.0 %collective-permute-done = bf16[64,2048]{1,0:T(8,128)(2,1)S(1)} collective-permute-done((bf16[64,2048]{1,0:T(8,128)(2,1)S(1)}, bf16[64,2048]{1,0:T(8,128)(2,1)S(1)}, u32[]{:S(2)}, u32[]{:S(2)}) %collective-permute-start) | collective-permute-done | bytes 262176 | tf_op jit(solution)/shard_map/ppermute | solution.py:76
  193.8 7.9 %psum.39 = f32[32]{0:T(128)S(1)} all-reduce(f32[32]{0:T(128)S(1)} %get-tuple-element.20), channel_id=1, replica_groups=mesh['hi'=2,'core'=2,'grp'=4,'z'=4,'xlo'=2] {'grp'}, use_global_device_ids=true, to_apply=%region_15.16 | all-reduce | flops 32 | bytes 256 | tf_op jit(solution)/shard_map/psum | solution.py:199
  207.0 3.7 %collective-permute-start.5 = (bf16[64,2048]{1,0:T(8,128)(2,1)S(1)}, bf16[64,2048]{1,0:T(8,128)(2,1)S(1)}, u32[]{:S(2)}, u32[]{:S(2)}) collective-permute-start(bf16[64,2048]{1,0:T(8,128)(2,1)S(1)} %maximum_select_fusion.2), channel_id=1, source_target_pairs={{0,64},{64,0},{1,65},{65,1},{2,66},{66,2},{3,67},{67,3},{4,68},{68... | collective-permute-start | bytes 786440 | tf_op jit(solution)/shard_map/ppermute | solution.py:39
  210.7 4.4 %collective-permute-done.5 = bf16[64,2048]{1,0:T(8,128)(2,1)S(1)} collective-permute-done((bf16[64,2048]{1,0:T(8,128)(2,1)S(1)}, bf16[64,2048]{1,0:T(8,128)(2,1)S(1)}, u32[]{:S(2)}, u32[]{:S(2)}) %collective-permute-start.5) | collective-permute-done | bytes 262176 | tf_op jit(solution)/shard_map/ppermute | solution.py:39
  221.1 9.6 %collective-permute-done.6 = bf16[128,2048]{1,0:T(8,128)(2,1)S(1)} collective-permute-done((bf16[128,2048]{1,0:T(8,128)(2,1)S(1)}, bf16[128,2048]{1,0:T(8,128)(2,1)S(1)}, u32[]{:S(2)}, u32[]{:S(2)}) %collective-permute-start.6) | collective-permute-done | bytes 524320 | tf_op jit(solution)/shard_map/ppermute | solution.py:62
  230.7 8.2 %collective-permute-done.7 = bf16[128,2048]{1,0:T(8,128)(2,1)S(1)} collective-permute-done((bf16[128,2048]{1,0:T(8,128)(2,1)S(1)}, bf16[128,2048]{1,0:T(8,128)(2,1)S(1)}, u32[]{:S(2)}, u32[]{:S(2)}) %collective-permute-start.7) | collective-permute-done | bytes 524320 | tf_op jit(solution)/shard_map/ppermute | solution.py:62
  241.2 5.2 %fusion.29 = bf16[512,896]{1,0:T(8,128)(2,1)S(1)} fusion(bf16[512,2048]{1,0:T(8,128)(2,1)} %bitcast.187, bf16[2048,448]{0,1:T(8,128)(2,1)} %collective-permute-done.10, bf16[2048,448]{0,1:T(8,128)(2,1)} %param.32), kind=kOutput, calls=%fused_computation.38 | convolution fusion | flops 1886846976 | bytes 6684672 | tf_op jit(solution)/shard_map/dot_general | solution.py:210
  246.4 3.9 %fusion.32 = bf16[512,896]{1,0:T(8,128)(2,1)S(1)} fusion(bf16[512,2048]{1,0:T(8,128)(2,1)S(1)} %bitcast.188, bf16[2048,448]{0,1:T(8,128)(2,1)} %collective-permute-done.9, bf16[2048,448]{0,1:T(8,128)(2,1)S(1)} %copy-done.9), kind=kOutput, calls=%fused_computation.39 | convolution fusion | flops 1886846976 | bytes 6684672 | tf_op jit(solution)/shard_map/dot_general | solution.py:209
  251.8 26.3 %reduce-scatter.5.cloned.1.call-done = bf16[128,1792]{1,0:T(8,128)(2,1)} async-done(((bf16[512,1792]{1,0:T(8,128)(2,1)}), bf16[128,1792]{1,0:T(8,128)(2,1)}) %reduce-scatter.5.cloned.1.call-update) | async-done | bytes 458768 | tf_op jit(solution)/shard_map/reduce_scatter | solution.py:212
  279.3 14.6 %all_gather.7 = bf16[512,896]{1,0:T(8,128)(2,1)S(1)} all-gather(bf16[128,896]{1,0:T(8,128)(2,1)S(1)} %fusion.44), channel_id=1, replica_groups=mesh['hi'=2,'core'=2,'grp'=4,'z'=4,'xlo'=2] {'grp'}, dimensions={0}, use_global_device_ids=true | all-gather | bytes 1146880 | tf_op jit(solution)/shard_map/all_gather | solution.py:216
  293.8 4.4 %fusion.20 = bf16[512,2048]{1,0:T(8,128)(2,1)S(1)} fusion(bf16[512,896]{1,0:T(8,128)(2,1)S(1)} %all_gather.7, bf16[448,2048]{1,0:T(8,128)(2,1)} %collective-permute-done.11, bf16[448,2048]{1,0:T(8,128)(2,1)} %param.33), kind=kOutput, calls=%fused_computation.28 | convolution fusion | flops 1887436800 | bytes 6684672 | tf_op jit(solution)/shard_map/dot_general | solution.py:217
  306.3 9.4 %collective-permute-done.12 = bf16[128,2048]{1,0:T(8,128)(2,1)} collective-permute-done((bf16[128,2048]{1,0:T(8,128)(2,1)}, bf16[128,2048]{1,0:T(8,128)(2,1)}, u32[]{:S(2)}, u32[]{:S(2)}) %collective-permute-start.12) | collective-permute-done | bytes 524320 | tf_op jit(solution)/shard_map/ppermute | solution.py:76
  315.7 8.8 %collective-permute-done.13 = bf16[128,2048]{1,0:T(8,128)(2,1)} collective-permute-done((bf16[128,2048]{1,0:T(8,128)(2,1)S(1)}, bf16[128,2048]{1,0:T(8,128)(2,1)}, u32[]{:S(2)}, u32[]{:S(2)}) %collective-permute-start.13) | collective-permute-done | bytes 524320 | tf_op jit(solution)/shard_map/ppermute | solution.py:76
  329.5 4.8 %collective-permute-done.15 = bf16[64,2048]{1,0:T(8,128)(2,1)S(1)} collective-permute-done((bf16[64,2048]{1,0:T(8,128)(2,1)S(1)}, bf16[64,2048]{1,0:T(8,128)(2,1)S(1)}, u32[]{:S(2)}, u32[]{:S(2)}) %collective-permute-start.15) | collective-permute-done | bytes 262176 | tf_op jit(solution)/shard_map/ppermute | solution.py:52
  (125 shorter events, 80.7 us)
Async XLA Ops:
  6.5 55.3 %copy-start = (bf16[2,4096,128]{2,1,0:T(8,128)(2,1)S(1)}, bf16[2,4096,128]{2,1,0:T(8,128)(2,1)}, u32[]{:S(2)}) copy-start(bf16[2,4096,128]{2,1,0:T(8,128)(2,1)} %param.24) | copy-start | bytes 6291460
  6.5 149.1 %reduce-scatter.3.cloned.1.call-start = ((), (), s32[]{:S(2)}) async-start(), calls=%async_computation.2 | async-start | bytes 1474560 | tf_op jit(solution)/shard_map/reduce_scatter | solution.py:176
  80.9 18.1 %copy-start.13 = (bf16[128]{0:T(256)(128)(2,1)S(1)}, bf16[128]{0:T(256)(128)(2,1)}, u32[]{:S(2)}) copy-start(bf16[128]{0:T(256)(128)(2,1)} %constant.153.clone.1) | copy-start | bytes 772
  130.6 147.5 %reduce-scatter.5.cloned.1.call-start = ((), (), s32[]{:S(2)}) async-start(), calls=%async_computation.3 | async-start | bytes 2293760 | tf_op jit(solution)/shard_map/reduce_scatter | solution.py:212
  173.8 15.4 %copy-start.4 = (bf16[256,2048]{1,0:T(8,128)(2,1)S(1)}, bf16[256,2048]{1,0:T(8,128)(2,1)}, u32[]{:S(2)}) copy-start(bf16[256,2048]{1,0:T(8,128)(2,1)} %param.18) | copy-start | bytes 3145732
  173.9 9.9 %collective-permute-start = (bf16[64,2048]{1,0:T(8,128)(2,1)S(1)}, bf16[64,2048]{1,0:T(8,128)(2,1)S(1)}, u32[]{:S(2)}, u32[]{:S(2)}) collective-permute-start(bf16[64,2048]{1,0:T(8,128)(2,1)S(1)} %get-tuple-element.27), channel_id=1, source_target_pairs={{0,2},{2,4},{4,6},{6,0},{1,3},{3,5},{5,7},{7,1},{8,10},{10,12},{12... | collective-permute-start | bytes 786440 | tf_op jit(solution)/shard_map/ppermute | solution.py:76
  175.5 11.0 %collective-permute-start.1 = (bf16[64,2048]{1,0:T(8,128)(2,1)S(1)}, bf16[64,2048]{1,0:T(8,128)(2,1)S(1)}, u32[]{:S(2)}, u32[]{:S(2)}) collective-permute-start(bf16[64,2048]{1,0:T(8,128)(2,1)S(1)} %get-tuple-element.29), channel_id=1, source_target_pairs={{0,4},{2,6},{4,0},{6,2},{1,5},{3,7},{5,1},{7,3},{8,12},{10,14},{12... | collective-permute-start | bytes 786440 | tf_op jit(solution)/shard_map/ppermute | solution.py:76
  178.3 8.2 %collective-permute-start.2 = (bf16[64,2048]{1,0:T(8,128)(2,1)S(1)}, bf16[64,2048]{1,0:T(8,128)(2,1)}, u32[]{:S(2)}, u32[]{:S(2)}) collective-permute-start(bf16[64,2048]{1,0:T(8,128)(2,1)S(1)} %get-tuple-element.28), channel_id=1, source_target_pairs={{0,6},{2,0},{4,2},{6,4},{1,7},{3,1},{5,3},{7,5},{8,14},{10,8},{12,... | collective-permute-start | bytes 786440 | tf_op jit(solution)/shard_map/ppermute | solution.py:76
  187.6 14.1 %copy-start.7 = (f32[2048]{0:T(1024)S(1)}, f32[2048]{0:T(1024)}, u32[]{:S(2)}) copy-start(f32[2048]{0:T(1024)} %param.30) | copy-start | bytes 24580
  187.7 5.0 %collective-permute-start.3 = (bf16[32,2048]{1,0:T(8,128)(2,1)S(1)}, bf16[32,2048]{1,0:T(8,128)(2,1)S(1)}, u32[]{:S(2)}, u32[]{:S(2)}) collective-permute-start(bf16[32,2048]{1,0:T(8,128)(2,1)S(1)} %fusion.52), channel_id=1, source_target_pairs={{0,1},{1,0},{2,3},{3,2},{4,5},{5,4},{6,7},{7,6},{8,9},{9,8},{10,11... | collective-permute-start | bytes 393224 | tf_op jit(solution)/shard_map/ppermute | solution.py:52
  189.2 51.9 %collective-permute-start.10 = (bf16[2048,448]{0,1:T(8,128)(2,1)}, bf16[2048,448]{0,1:T(8,128)(2,1)}, u32[]{:S(2)}, u32[]{:S(2)}) collective-permute-start(bf16[2048,448]{0,1:T(8,128)(2,1)} %param.32), channel_id=1, source_target_pairs={{0,32},{32,0},{1,33},{33,1},{2,34},{34,2},{3,35},{35,3},{4,36},{36... | collective-permute-start | bytes 5505032 | tf_op jit(solution)/shard_map/ppermute | solution.py:204
  201.9 5.0 %collective-permute-start.4 = (bf16[32,2048]{1,0:T(8,128)(2,1)S(1)}, bf16[32,2048]{1,0:T(8,128)(2,1)S(1)}, u32[]{:S(2)}, u32[]{:S(2)}) collective-permute-start(bf16[32,2048]{1,0:T(8,128)(2,1)S(1)} %fusion.47), channel_id=1, source_target_pairs={{0,1},{1,0},{2,3},{3,2},{4,5},{5,4},{6,7},{7,6},{8,9},{9,8},{10,11... | collective-permute-start | bytes 393224 | tf_op jit(solution)/shard_map/ppermute | solution.py:39
  203.5 42.9 %collective-permute-start.9 = (bf16[2048,448]{0,1:T(8,128)(2,1)}, bf16[2048,448]{0,1:T(8,128)(2,1)}, u32[]{:S(2)}, u32[]{:S(2)}) collective-permute-start(bf16[2048,448]{0,1:T(8,128)(2,1)} %param.31), channel_id=1, source_target_pairs={{0,32},{32,0},{1,33},{33,1},{2,34},{34,2},{3,35},{35,3},{4,36},{36... | collective-permute-start | bytes 5505032 | tf_op jit(solution)/shard_map/ppermute | solution.py:203
  207.0 8.2 %collective-permute-start.5 = (bf16[64,2048]{1,0:T(8,128)(2,1)S(1)}, bf16[64,2048]{1,0:T(8,128)(2,1)S(1)}, u32[]{:S(2)}, u32[]{:S(2)}) collective-permute-start(bf16[64,2048]{1,0:T(8,128)(2,1)S(1)} %maximum_select_fusion.2), channel_id=1, source_target_pairs={{0,64},{64,0},{1,65},{65,1},{2,66},{66,2},{3,67},{67,3},{4,68},{68... | collective-permute-start | bytes 786440 | tf_op jit(solution)/shard_map/ppermute | solution.py:39
  215.2 15.4 %collective-permute-start.6 = (bf16[128,2048]{1,0:T(8,128)(2,1)S(1)}, bf16[128,2048]{1,0:T(8,128)(2,1)S(1)}, u32[]{:S(2)}, u32[]{:S(2)}) collective-permute-start(bf16[128,2048]{1,0:T(8,128)(2,1)S(1)} %maximum_select_fusion.1), channel_id=1, source_target_pairs={{0,2},{2,4},{4,6},{6,0},{1,3},{3,5},{5,7},{7,1},{8,10},{10,12},{12... | collective-permute-start | bytes 1572872 | tf_op jit(solution)/shard_map/ppermute | solution.py:62
  217.2 21.7 %collective-permute-start.7 = (bf16[128,2048]{1,0:T(8,128)(2,1)S(1)}, bf16[128,2048]{1,0:T(8,128)(2,1)S(1)}, u32[]{:S(2)}, u32[]{:S(2)}) collective-permute-start(bf16[128,2048]{1,0:T(8,128)(2,1)S(1)} %maximum_select_fusion.1), channel_id=1, source_target_pairs={{0,4},{2,6},{4,0},{6,2},{1,5},{3,7},{5,1},{7,3},{8,12},{10,14},{12... | collective-permute-start | bytes 1572872 | tf_op jit(solution)/shard_map/ppermute | solution.py:62
  219.3 19.5 %collective-permute-start.8 = (bf16[128,2048]{1,0:T(8,128)(2,1)S(1)}, bf16[128,2048]{1,0:T(8,128)(2,1)S(1)}, u32[]{:S(2)}, u32[]{:S(2)}) collective-permute-start(bf16[128,2048]{1,0:T(8,128)(2,1)S(1)} %maximum_select_fusion.1), channel_id=1, source_target_pairs={{0,6},{2,0},{4,2},{6,4},{1,7},{3,1},{5,3},{7,5},{8,14},{10,8},{12,... | collective-permute-start | bytes 1572872 | tf_op jit(solution)/shard_map/ppermute | solution.py:62
  251.7 42.1 %collective-permute-start.11 = (bf16[448,2048]{1,0:T(8,128)(2,1)}, bf16[448,2048]{1,0:T(8,128)(2,1)}, u32[]{:S(2)}, u32[]{:S(2)}) collective-permute-start(bf16[448,2048]{1,0:T(8,128)(2,1)} %param.33), channel_id=1, source_target_pairs={{0,32},{32,0},{1,33},{33,1},{2,34},{34,2},{3,35},{35,3},{4,36},{36... | collective-permute-start | bytes 5505032 | tf_op jit(solution)/shard_map/ppermute | solution.py:205
  300.5 15.2 %collective-permute-start.12 = (bf16[128,2048]{1,0:T(8,128)(2,1)}, bf16[128,2048]{1,0:T(8,128)(2,1)}, u32[]{:S(2)}, u32[]{:S(2)}) collective-permute-start(bf16[128,2048]{1,0:T(8,128)(2,1)} %get-tuple-element.24), channel_id=1, source_target_pairs={{0,2},{2,4},{4,6},{6,0},{1,3},{3,5},{5,7},{7,1},{8,10},{10,12},{12... | collective-permute-start | bytes 1572872 | tf_op jit(solution)/shard_map/ppermute | solution.py:76
  302.1 22.4 %collective-permute-start.13 = (bf16[128,2048]{1,0:T(8,128)(2,1)S(1)}, bf16[128,2048]{1,0:T(8,128)(2,1)}, u32[]{:S(2)}, u32[]{:S(2)}) collective-permute-start(bf16[128,2048]{1,0:T(8,128)(2,1)S(1)} %get-tuple-element.26), channel_id=1, source_target_pairs={{0,4},{2,6},{4,0},{6,2},{1,5},{3,7},{5,1},{7,3},{8,12},{10,14},{12... | collective-permute-start | bytes 1572872 | tf_op jit(solution)/shard_map/ppermute | solution.py:76
  304.9 19.6 %collective-permute-start.14 = (bf16[128,2048]{1,0:T(8,128)(2,1)S(1)}, bf16[128,2048]{1,0:T(8,128)(2,1)}, u32[]{:S(2)}, u32[]{:S(2)}) collective-permute-start(bf16[128,2048]{1,0:T(8,128)(2,1)S(1)} %get-tuple-element.25), channel_id=1, source_target_pairs={{0,6},{2,0},{4,2},{6,4},{1,7},{3,1},{5,3},{7,5},{8,14},{10,8},{12,... | collective-permute-start | bytes 1572872 | tf_op jit(solution)/shard_map/ppermute | solution.py:76
  306.3 33.9 %copy-start.1 = (bf16[2,4096,128]{2,1,0:T(8,128)(2,1)S(1)}, bf16[2,4096,128]{2,1,0:T(8,128)(2,1)}, u32[]{:S(2)}) copy-start(bf16[2,4096,128]{2,1,0:T(8,128)(2,1)} %param.24) | copy-start | bytes 6291460
  326.4 8.0 %collective-permute-start.15 = (bf16[64,2048]{1,0:T(8,128)(2,1)S(1)}, bf16[64,2048]{1,0:T(8,128)(2,1)S(1)}, u32[]{:S(2)}, u32[]{:S(2)}) collective-permute-start(bf16[64,2048]{1,0:T(8,128)(2,1)S(1)} %dynamic-slice_bitcast_fusion.3), channel_id=1, source_target_pairs={{0,64},{64,0},{1,65},{65,1},{2,66},{66,2},{3,67},{67,3},{4,68},{68... | collective-permute-start | bytes 786440 | tf_op jit(solution)/shard_map/ppermute | solution.py:52
  334.4 5.0 %collective-permute-start.16 = (bf16[32,2048]{1,0:T(8,128)(2,1)S(1)}, bf16[32,2048]{1,0:T(8,128)(2,1)S(1)}, u32[]{:S(2)}, u32[]{:S(2)}) collective-permute-start(bf16[32,2048]{1,0:T(8,128)(2,1)S(1)} %dynamic-slice_bitcast_fusion.7), channel_id=1, source_target_pairs={{0,1},{1,0},{2,3},{3,2},{4,5},{5,4},{6,7},{7,6},{8,9},{9,8},{10,11... | collective-permute-start | bytes 393224 | tf_op jit(solution)/shard_map/ppermute | solution.py:52
  (9 other events, 28.2 us)
Sparse Core Ops, SparseCore 0:
  130.7 24.8 reduce-scatter.2
  251.8 26.1 reduce-scatter.4
